TPU v7x, 1024 devices: a whole 4x4x32 slice. The times are simulated.
1024 devices in a mesh: rel: 8 (over y, core), vrow: 32 (over z), vcol: 4 (over x).
Axes of the slice: x: 4, y: 4, z: 32, core: 2. Of those that a mesh axis runs over, the one named last changes fastest.
Arguments:
- features: bfloat16 [16384, 1024], P('vrow'), may hold values from -6 to 6
- first_weight: bfloat16 [16, 1024, 512], P('rel'), may hold values from -0.1875 to 0.1875
- first_root: bfloat16 [1024, 512], replicated, may hold values from -0.1875 to 0.1875
- first_bias: float32 [512], replicated, may hold values from -3 to 3
- second_weight: bfloat16 [16, 512, 512], P('rel'), may hold values from -0.25 to 0.25
- second_root: bfloat16 [512, 512], replicated, may hold values from -0.25 to 0.25
- second_bias: float32 [512], replicated, may hold values from -3 to 3
- tiles: bfloat16 [16, 128, 12, 128, 128], P('rel', 'vrow', 'vcol')
- tile_source: int32 [16, 128, 12], P('rel', 'vrow', 'vcol'), may hold values from 0 to 5, as said below
- tile_count: int32 [16, 128, 4], P('rel', 'vrow', 'vcol'), may hold values from 1 to 3, as said below
- send_rows: int32 [8, 32, 4, 256], P('rel', 'vrow', 'vcol'), may hold values from 0 to 511
Outputs:
- embeddings: bfloat16 [32, 512, 512], P('vrow', ('rel', 'vcol'))
Inputs may be any that keep to these rules, and one draw needn't show every extreme that they name: `tile_source`: the first of every column group's 3 tile slots names a block of received rows (4 or more). `tile_count`: each relation has a level of its own that bounds its counts; in every draw some block row of some relation fills all 3 slots of every column group.
All inputs are finite; a program needn't handle non-finite values.
Results may differ from a plain program's by a relative error of at most 0.0055.
Values may be sent and summed in bfloat16 or wider, within the bound.
No kernel may reach another device: no remote copies, remote signals or barrier semaphores. Data moves between devices by JAX's collectives and lax.ppermute only.
A program may use at most 32 MiB of HBM per device.

v0:
```python
import jax
import jax.numpy as jnp
from jax import lax
from jax.sharding import PartitionSpec as P


def project(row_values, weight):
    return jnp.einsum("nf,sfh->nsh", row_values, weight, preferred_element_type=jnp.float32).astype(
        jnp.bfloat16
    )


def gather_blocks(sources, tile_source, block_size):
    block_count = sources.shape[0] // block_size
    blocks = sources.reshape(block_count, block_size, sources.shape[1], sources.shape[2])

    def pick(source_blocks, indices):
        return source_blocks[indices]

    return jax.vmap(pick, in_axes=(2, 0))(blocks, tile_source)


def aggregate(sources, masked, tile_source):
    picked = gather_blocks(sources, tile_source, masked.shape[-1])
    summed = jnp.einsum("sktab,sktbh->kah", masked, picked, preferred_element_type=jnp.float32)
    return summed.reshape(-1, summed.shape[-1])


def fetch_first(values, send_index):
    outgoing = jnp.take(values, send_index, axis=0)
    return lax.all_to_all(outgoing, "vrow", split_axis=0, concat_axis=0, tiled=True)


def fetch_second(values, send_index):
    outgoing = jnp.take(values, send_index, axis=0)
    return lax.all_to_all(outgoing, "vrow", split_axis=0, concat_axis=0, tiled=True)


def body(
    features,
    first_weight,
    first_root,
    first_bias,
    second_weight,
    second_root,
    second_bias,
    tiles,
    tile_source,
    tile_count,
    send_rows,
):
    local_rows = features.shape[0]
    send_index = send_rows.reshape(-1)
    tile_slots = tiles.shape[2]
    live_tiles = (jnp.arange(tile_slots, dtype=jnp.int32)[None, None, :] < tile_count).astype(
        tiles.dtype
    )
    masked = tiles * live_tiles[:, :, :, None, None]
    share_rows = local_rows // lax.axis_size(("rel", "vcol"))
    received = fetch_first(features, send_index)
    first_proj = project(jnp.concatenate([features, received], axis=0), first_weight)
    first_part = aggregate(first_proj, masked, tile_source)
    first_total = lax.psum(first_part.astype(jnp.bfloat16), ("rel", "vcol")).astype(jnp.float32)
    root_term = jnp.dot(features, first_root, preferred_element_type=jnp.float32)
    hidden = jax.nn.relu(first_total + root_term + first_bias).astype(jnp.bfloat16)
    received_hidden = fetch_second(hidden, send_index)
    second_proj = project(jnp.concatenate([hidden, received_hidden], axis=0), second_weight)
    second_part = aggregate(second_proj, masked, tile_source)
    second_share = lax.psum_scatter(second_part, ("rel", "vcol"), scatter_dimension=0, tiled=True)
    row_start = lax.axis_index(("rel", "vcol")) * share_rows
    own_hidden = lax.dynamic_slice_in_dim(hidden, row_start, share_rows, 0)
    second_term = jnp.dot(own_hidden, second_root, preferred_element_type=jnp.float32)
    result = jax.nn.relu(second_share + second_term + second_bias).astype(jnp.bfloat16)
    return result[None]


def solution(mesh):
    in_specs = (
        P("vrow", None),
        P("rel", None, None),
        P(),
        P(),
        P("rel", None, None),
        P(),
        P(),
        P("rel", "vrow", "vcol", None, None),
        P("rel", "vrow", "vcol"),
        P("rel", "vrow", "vcol"),
        P("rel", "vrow", "vcol", None),
    )
    out_specs = P("vrow", ("rel", "vcol"), None)
    return jax.shard_map(body, mesh=mesh, in_specs=in_specs, out_specs=out_specs, check_vma=False)
```

profile of v0, /device:TPU:1, one launch (start us, length us, event | category | flops | bytes accessed | tf_op | source)
XLA Modules:
  0.0 479.0 jit_solution(1828485406668377916)
XLA Ops:
  6.5 0.0 copy-start
  6.5 0.8 compare_select_fusion.2
  7.4 0.5 broadcast.96
  7.9 1.3 reduce.3
  9.2 0.1 reshape.71
  9.3 0.0 copy-start.4
  9.3 0.0 copy-start.6
  9.4 0.0 copy-start.1
  9.4 3.8 gather_fusion
  13.2 1.9 bitcast_select_fusion
  15.1 29.4 %all-to-all-start = ((bf16[32,8,1024]{2,1,0:T(8,128)(2,1)}), bf16[32,8,1024]{2,1,0:T(8,128)(2,1)}, u32[]{:S(2)}, u32[]{:S(2)}) async-start(bf16[32,8,1024]{2,1,0:T(8,128)(2,1)} %bitcast_select_fusion), calls=%async_computation | async-start | bytes 1048576 | tf_op jit(solution)/shard_map/all_to_all | solution.py:31
  44.5 0.0 all-reduce.2.cloned.1.call-start
  44.6 0.0 copy-done.4
  44.6 0.1 copy.15
  44.7 0.1 reshape.92
  44.8 0.0 copy-done.6
  44.8 0.1 fusion.18
  44.9 64.0 %all-to-all-done = bf16[32,8,1024]{2,1,0:T(8,128)(2,1)} async-done(((bf16[32,8,1024]{2,1,0:T(8,128)(2,1)}), bf16[32,8,1024]{2,1,0:T(8,128)(2,1)}, u32[]{:S(2)}, u32[]{:S(2)}) %all-to-all-start) | async-done | bytes 524320 | tf_op jit(solution)/shard_map/all_to_all | solution.py:31
  108.8 0.0 copy-done
  108.8 0.0 copy-done.1
  108.8 4.0 convolution_convert_fusion.1
  112.8 3.9 gather_fusion.2
  116.7 0.0 copy-start.7
  116.7 3.6 fusion.4
  120.3 0.0 all-reduce.2.cloned.1.call-update
  120.3 0.0 reduce-scatter.2.cloned.1.call-start
  120.3 158.6 %all-reduce.2.cloned.1.call-done = bf16[512,512]{1,0:T(8,128)(2,1)} async-done(((bf16[512,512]{1,0:T(8,128)(2,1)}), bf16[512,512]{1,0:T(8,128)(2,1)}) %all-reduce.2.cloned.1.call-update) | async-done | bytes 524304 | tf_op jit(solution)/shard_map/psum | solution.py:63
  278.9 0.0 copy-done.7
  278.9 2.9 fusion.5
  281.8 0.0 copy-start.2
  281.8 2.4 gather_fusion.1
  284.2 0.1 bitcast_select_fusion.1
  284.3 63.0 %all_to_all.18 = bf16[32,8,512]{2,1,0:T(8,128)(2,1)S(1)} all-to-all(bf16[32,8,512]{2,1,0:T(8,128)(2,1)S(1)} %bitcast_select_fusion.1), channel_id=1, replica_groups=mesh['rel'=8,'vrow'=32,'vcol'=4] {'vrow'}, dimensions={0} | all-to-all | bytes 524288 | tf_op jit(solution)/shard_map/all_to_all | solution.py:36
  347.3 0.0 copy-done.2
  347.3 3.4 convolution_convert_fusion
  350.7 0.0 copy-start.3
  350.7 3.9 gather_fusion.3
  354.6 0.0 copy-start.5
  354.6 0.0 copy-done.3
  354.6 3.5 fusion.12
  358.1 0.0 reduce-scatter.2.cloned.1.call-update
  358.1 112.2 %reduce-scatter.2.cloned.1.call-done = f32[16,512]{1,0:T(8,128)} async-done(((f32[512,512]{1,0:T(8,128)}), f32[16,512]{1,0:T(8,128)}) %reduce-scatter.2.cloned.1.call-update) | async-done | bytes 32784 | tf_op jit(solution)/shard_map/reduce_scatter | solution.py:69
  470.3 0.0 copy-done.5
  470.3 1.8 fusion.9
  (3 shorter events, 0.0 us)
Async XLA Ops:
  6.5 102.3 %copy-start = (bf16[2,1024,512]{2,1,0:T(8,128)(2,1)S(1)}, bf16[2,1024,512]{2,1,0:T(8,128)(2,1)}, u32[]{:S(2)}) copy-start(bf16[2,1024,512]{2,1,0:T(8,128)(2,1)} %param.12) | copy-start | bytes 6291460
  9.3 35.2 %copy-start.4 = (s32[2,4,3]{1,0,2:T(2,128)S(1)}, s32[2,4,3]{1,0,2:T(2,128)}, u32[]{:S(2)}) copy-start(s32[2,4,3]{1,0,2:T(2,128)} %param.19) | copy-start | bytes 292
  9.3 35.4 %copy-start.6 = (s32[2,4,1]{1,2,0:T(1,128)S(1)}, s32[2,4,1]{1,2,0:T(1,128)}, u32[]{:S(2)}) copy-start(s32[2,4,1]{1,2,0:T(1,128)} %param.20) | copy-start | bytes 100
  9.4 99.5 %copy-start.1 = (bf16[512,1024]{1,0:T(8,128)(2,1)S(1)}, bf16[512,1024]{1,0:T(8,128)(2,1)}, u32[]{:S(2)}) copy-start(bf16[512,1024]{1,0:T(8,128)(2,1)} %param.11) | copy-start | bytes 3145732
  15.1 93.7 %all-to-all-start = ((bf16[32,8,1024]{2,1,0:T(8,128)(2,1)}), bf16[32,8,1024]{2,1,0:T(8,128)(2,1)}, u32[]{:S(2)}, u32[]{:S(2)}) async-start(bf16[32,8,1024]{2,1,0:T(8,128)(2,1)} %bitcast_select_fusion), calls=%async_computation | async-start | bytes 1048576 | tf_op jit(solution)/shard_map/all_to_all | solution.py:31
  44.5 234.4 %all-reduce.2.cloned.1.call-start = ((), (), s32[]{:S(2)}) async-start(), calls=%async_computation.3 | async-start | bytes 1048576 | tf_op jit(solution)/shard_map/psum | solution.py:63
  116.7 162.2 %copy-start.7 = (f32[512]{0:T(512)S(1)}, f32[512]{0:T(512)}, u32[]{:S(2)}) copy-start(f32[512]{0:T(512)} %param.14) | copy-start | bytes 6148
  120.3 350.1 %reduce-scatter.2.cloned.1.call-start = ((), (), s32[]{:S(2)}) async-start(), calls=%async_computation.4 | async-start | bytes 1081344 | tf_op jit(solution)/shard_map/reduce_scatter | solution.py:69
  281.8 65.5 %copy-start.2 = (bf16[512,512]{1,0:T(8,128)(2,1)S(1)}, bf16[512,512]{1,0:T(8,128)(2,1)}, u32[]{:S(2)}) copy-start(bf16[512,512]{1,0:T(8,128)(2,1)} %fusion.5) | copy-start | bytes 1572868
  350.7 4.0 copy-start.3
  354.6 115.7 %copy-start.5 = (f32[512]{0:T(512)S(1)}, f32[512]{0:T(512)}, u32[]{:S(2)}) copy-start(f32[512]{0:T(512)} %param.17) | copy-start | bytes 6148
Sparse Core Ops, SparseCore 0:
  120.4 158.4 all-reduce.1
  358.3 112.0 reduce-scatter.1
where the time goes:
time: 480 us; the launch traced here: 479 us
  waiting for transfers between devices  335 us (70%)
  blocking collectives  63 us (13%)
  starting transfers between devices  29.5 us (6%)
  matrix products  19.1 us (4%)
  local copies, waits for them, and re-layouts  14.8 us (3%)
  between operations  13.5 us (3%)
    psum x1, waiting for transfers between devices, body(): lax.psum(first_part.astype(jnp.bfloat16), ('rel', 'vcol'))  159 us
    reduce_scatter x1, waiting for transfers between devices, body(): lax.psum_scatter(second_part, ('rel', 'vcol'), scatter_dimension=0, tiled...  112 us
    all_to_all x1, waiting for transfers between devices, fetch_first(): lax.all_to_all(outgoing, 'vrow', split_axis=0, concat_axis=0, tiled=True)  64 us
    all_to_all x1, blocking collectives, fetch_second(): lax.all_to_all(outgoing, 'vrow', split_axis=0, concat_axis=0, tiled=True)  63 us
    all_to_all x1, starting transfers between devices, fetch_first(): lax.all_to_all(outgoing, 'vrow', split_axis=0, concat_axis=0, tiled=True)  29.4 us
  transfers between devices with their start and end apart: 3, of which 3 were waited for; matrix products, arithmetic and copies ran while one was open for 0% of the time, Pallas kernels for 0%

commit v1 on v0

--- a/solution.py
+++ b/solution.py
@@ -2,6 +2,9 @@
 import jax.numpy as jnp
 from jax import lax
 from jax.sharding import PartitionSpec as P
+
+
+GROUP = ("rel", "vcol")
 
 
 def project(row_values, weight):
@@ -26,14 +29,21 @@
     return summed.reshape(-1, summed.shape[-1])
 
 
-def fetch_first(values, send_index):
+def fetch_rows(values, send_index):
     outgoing = jnp.take(values, send_index, axis=0)
     return lax.all_to_all(outgoing, "vrow", split_axis=0, concat_axis=0, tiled=True)
 
 
-def fetch_second(values, send_index):
-    outgoing = jnp.take(values, send_index, axis=0)
-    return lax.all_to_all(outgoing, "vrow", split_axis=0, concat_axis=0, tiled=True)
+def scatter_sum(part, parts):
+    chunks = part.reshape(parts, part.shape[0] // parts, part.shape[1])
+    received = lax.all_to_all(chunks, GROUP, 0, 0, tiled=False)
+    return jnp.sum(received.astype(jnp.float32), axis=0)
+
+
+def gather_all(share, parts):
+    copies = jnp.broadcast_to(share[None], (parts,) + share.shape)
+    received = lax.all_to_all(copies, GROUP, 0, 0, tiled=False)
+    return received.reshape(parts * share.shape[0], share.shape[1])
 
 
 def body(
@@ -56,20 +66,22 @@
         tiles.dtype
     )
     masked = tiles * live_tiles[:, :, :, None, None]
-    share_rows = local_rows // lax.axis_size(("rel", "vcol"))
-    received = fetch_first(features, send_index)
+    parts = lax.axis_size(GROUP)
+    share_rows = local_rows // parts
+    row_start = lax.axis_index(GROUP) * share_rows
+    received = fetch_rows(features, send_index)
     first_proj = project(jnp.concatenate([features, received], axis=0), first_weight)
     first_part = aggregate(first_proj, masked, tile_source)
-    first_total = lax.psum(first_part.astype(jnp.bfloat16), ("rel", "vcol")).astype(jnp.float32)
-    root_term = jnp.dot(features, first_root, preferred_element_type=jnp.float32)
-    hidden = jax.nn.relu(first_total + root_term + first_bias).astype(jnp.bfloat16)
-    received_hidden = fetch_second(hidden, send_index)
+    first_share = scatter_sum(first_part.astype(jnp.bfloat16), parts)
+    own_features = lax.dynamic_slice_in_dim(features, row_start, share_rows, 0)
+    first_term = jnp.dot(own_features, first_root, preferred_element_type=jnp.float32)
+    hidden_share = jax.nn.relu(first_share + first_term + first_bias).astype(jnp.bfloat16)
+    hidden = gather_all(hidden_share, parts)
+    received_hidden = fetch_rows(hidden, send_index)
     second_proj = project(jnp.concatenate([hidden, received_hidden], axis=0), second_weight)
     second_part = aggregate(second_proj, masked, tile_source)
-    second_share = lax.psum_scatter(second_part, ("rel", "vcol"), scatter_dimension=0, tiled=True)
-    row_start = lax.axis_index(("rel", "vcol")) * share_rows
-    own_hidden = lax.dynamic_slice_in_dim(hidden, row_start, share_rows, 0)
-    second_term = jnp.dot(own_hidden, second_root, preferred_element_type=jnp.float32)
+    second_share = scatter_sum(second_part, parts)
+    second_term = jnp.dot(hidden_share, second_root, preferred_element_type=jnp.float32)
     result = jax.nn.relu(second_share + second_term + second_bias).astype(jnp.bfloat16)
     return result[None]
 
@@ -88,5 +100,5 @@
         P("rel", "vrow", "vcol"),
         P("rel", "vrow", "vcol", None),
     )
-    out_specs = P("vrow", ("rel", "vcol"), None)
+    out_specs = P("vrow", GROUP, None)
     return jax.shard_map(body, mesh=mesh, in_specs=in_specs, out_specs=out_specs, check_vma=False)

time: 480 us -> 232 us (0.48)
  waiting for transfers between devices: 335 us -> 75.5 us
  blocking collectives: 63 us -> 81.4 us
  between operations: 13.5 us -> 0.13 us
  starting transfers between devices: 29.5 us -> 38 us
    psum x1 -> x0, waiting for transfers between devices: 159 us -> none  [body(): lax.psum(first_part.astype(jnp.bfloat16), ('rel', 'vcol'))]
    reduce_scatter x1 -> x0, waiting for transfers between devices: 112 us -> none  [body(): lax.psum_scatter(second_part, ('rel', 'vcol'), scatter_dimension=0, tiled...]
    all_to_all x1 -> x3, blocking collectives: 63 us -> 81.4 us  [the longest x1 44.8 us: fetch_rows(): lax.all_to_all(outgoing, 'vrow', split_axis=0, concat_axis=0, tiled=True)]
    all_to_all x1 -> x2, waiting for transfers between devices: 64 us -> 75.5 us  [the longest x1 64 us: fetch_rows(): lax.all_to_all(outgoing, 'vrow', split_axis=0, concat_axis=0, tiled=True)]
    all_to_all x1 -> x2, starting transfers between devices: 29.4 us -> 38 us  [the longest x1 29.4 us: fetch_rows(): lax.all_to_all(outgoing, 'vrow', split_axis=0, concat_axis=0, tiled=True)]
  transfers between devices with their start and end apart: 3 -> 2, of which waited for: 3 -> 2; matrix products, arithmetic and copies ran while one was open for 0% -> 0% of each run, Pallas kernels for 0% -> 0%
where the time goes in v1:
time: 232 us; the launch traced here: 231 us
  blocking collectives  81.4 us (35%)
  waiting for transfers between devices  75.5 us (33%)
  starting transfers between devices  38 us (16%)
  matrix products  16.7 us (7%)
  local copies, waits for them, and re-layouts  13.6 us (6%)
  other arithmetic  5.53 us (2%)
    all_to_all x1, waiting for transfers between devices, fetch_rows(): lax.all_to_all(outgoing, 'vrow', split_axis=0, concat_axis=0, tiled=True)  64 us
    all_to_all x1, blocking collectives, fetch_rows(): lax.all_to_all(outgoing, 'vrow', split_axis=0, concat_axis=0, tiled=True)  44.8 us
    all_to_all x1, starting transfers between devices, fetch_rows(): lax.all_to_all(outgoing, 'vrow', split_axis=0, concat_axis=0, tiled=True)  29.4 us
    all_to_all x1, blocking collectives, scatter_sum(): received = lax.all_to_all(chunks, GROUP, 0, 0, tiled=False)  21.1 us
    all_to_all x1, blocking collectives, gather_all(): received = lax.all_to_all(copies, GROUP, 0, 0, tiled=False)  15.5 us
    all_to_all x1, waiting for transfers between devices, scatter_sum(): received = lax.all_to_all(chunks, GROUP, 0, 0, tiled=False)  11.5 us
    all_to_all x1, starting transfers between devices, scatter_sum(): received = lax.all_to_all(chunks, GROUP, 0, 0, tiled=False)  8.61 us
    gather x4, local copies, waits for them, and re-layouts, pick(): return source_blocks[indices]  8.02 us
  transfers between devices with their start and end apart: 2, of which 2 were waited for; matrix products, arithmetic and copies ran while one was open for 0% of the time, Pallas kernels for 0%

profile of v1, /device:TPU:1, one launch (start us, length us, event | category | flops | bytes accessed | tf_op | source)
XLA Modules:
  0.0 230.9 jit_solution(3166899036181410996)
XLA Ops:
  0.0 0.0 copy-start
  0.0 0.8 compare_select_fusion.2
  0.8 0.5 broadcast.97
  1.3 1.3 reduce.3
  2.7 0.1 reshape.74
  2.8 0.0 copy-start.3
  2.8 0.0 copy-start.6
  2.8 0.0 copy-start.1
  2.8 3.8 %gather_fusion = bf16[256,1024]{1,0:T(8,128)(2,1)} fusion(bf16[512,1024]{1,0:T(8,128)(2,1)} %param.11, s32[1024]{0:T(1024)S(1)} %pad_clamp_fusion), kind=kCustom, calls=%fused_computation | custom fusion | bytes 1049600 | tf_op jit(solution)/shard_map/jit(_take)/gather | solution.py:33
  6.6 2.0 bitcast_select_fusion
  8.6 29.4 %all-to-all-start = ((bf16[32,8,1024]{2,1,0:T(8,128)(2,1)}), bf16[32,8,1024]{2,1,0:T(8,128)(2,1)}, u32[]{:S(2)}, u32[]{:S(2)}) async-start(bf16[32,8,1024]{2,1,0:T(8,128)(2,1)} %bitcast_select_fusion), calls=%async_computation | async-start | bytes 1048576 | tf_op jit(solution)/shard_map/all_to_all | solution.py:34
  38.0 0.0 copy-done.3
  38.0 0.1 copy.15
  38.1 0.1 reshape.95
  38.2 0.0 copy-done.6
  38.2 0.1 fusion.18
  38.3 64.0 %all-to-all-done = bf16[32,8,1024]{2,1,0:T(8,128)(2,1)} async-done(((bf16[32,8,1024]{2,1,0:T(8,128)(2,1)}), bf16[32,8,1024]{2,1,0:T(8,128)(2,1)}, u32[]{:S(2)}, u32[]{:S(2)}) %all-to-all-start) | async-done | bytes 524320 | tf_op jit(solution)/shard_map/all_to_all | solution.py:34
  102.3 0.0 copy-done
  102.3 0.0 copy-done.1
  102.3 4.0 %convolution_convert_fusion.1 = bf16[768,2,512]{2,0,1:T(8,128)(2,1)} fusion(bf16[2,1024,512]{2,1,0:T(8,128)(2,1)S(1)} %copy-done, bf16[256,1024]{1,0:T(8,128)(2,1)} %bitcast.4, bf16[512,1024]{1,0:T(8,128)(2,1)S(1)} %copy-done.1), kind=kOutput, calls=%fused_computation.5 | convolution fusion | flops 1614544896 | bytes 5242880 | tf_op jit(solution)/shard_map/nf,sfh->nsh/dot_general | solution.py:11
  106.3 3.9 %gather_fusion.2 = bf16[24,128,512]{2,1,0:T(8,128)(2,1)} fusion(bf16[2,6,128,512]{3,2,1,0:T(8,128)(2,1)} %bitcast.57, s32[24]{0:T(128)S(1)} %reshape.95), kind=kCustom, calls=%fused_computation.2 | custom fusion | bytes 6291648 | tf_op jit(solution)/shard_map/vmap()/gather | solution.py:21
  110.2 0.0 copy-start.4
  110.2 3.6 %fusion.2 = bf16[4,128,512]{2,1,0:T(8,128)(2,1)} fusion(bf16[2,4,3,128,512]{4,3,2,1,0:T(8,128)(2,1)} %bitcast.55, bf16[2,4,3,128,128]{4,3,2,1,0:T(8,128)(2,1)} %param.18, bf16[2,4,3]{2,1,0:T(4,128)(2,1)S(1)} %fusion.18), kind=kOutput, calls=%fused_computation.10 | convolution fusion | flops 403308544 | bytes 4456496 | tf_op jit(solution)/shard_map/sktab,sktbh->kah/dot_general | solution.py:28
  113.7 8.6 %all-to-all-start.1 = ((bf16[32,16,512]{2,1,0:T(8,128)(2,1)}), bf16[32,16,512]{2,1,0:T(8,128)(2,1)}, u32[]{:S(2)}, u32[]{:S(2)}) async-start(bf16[32,16,512]{2,1,0:T(8,128)(2,1)} %bitcast.59), calls=%async_computation.1 | async-start | bytes 1048576 | tf_op jit(solution)/shard_map/all_to_all | solution.py:39
  122.4 11.5 %all-to-all-done.1 = bf16[32,16,512]{2,1,0:T(8,128)(2,1)} async-done(((bf16[32,16,512]{2,1,0:T(8,128)(2,1)}), bf16[32,16,512]{2,1,0:T(8,128)(2,1)}, u32[]{:S(2)}, u32[]{:S(2)}) %all-to-all-start.1) | async-done | bytes 524320 | tf_op jit(solution)/shard_map/all_to_all | solution.py:39
  133.8 1.1 convert_reduce_fusion
  135.0 0.0 copy-done.4
  135.0 1.5 fusion.8
  136.5 0.1 broadcast_in_dim.40
  136.5 15.5 %all_to_all.33 = bf16[32,16,512]{2,1,0:T(8,128)(2,1)S(1)} all-to-all(bf16[32,16,512]{2,1,0:T(8,128)(2,1)S(1)} %broadcast_in_dim.40), channel_id=1, replica_groups=mesh['rel'=8,'vrow'=32,'vcol'=4] {'rel','vcol'}, dimensions={0} | all-to-all | bytes 1048576 | tf_op jit(solution)/shard_map/all_to_all | solution.py:45
  152.0 1.2 gather_fusion.1
  153.2 0.1 bitcast_select_fusion.1
  153.3 44.8 %all_to_all.34 = bf16[32,8,512]{2,1,0:T(8,128)(2,1)S(1)} all-to-all(bf16[32,8,512]{2,1,0:T(8,128)(2,1)S(1)} %bitcast_select_fusion.1), channel_id=1, replica_groups=mesh['rel'=8,'vrow'=32,'vcol'=4] {'vrow'}, dimensions={0} | all-to-all | bytes 524288 | tf_op jit(solution)/shard_map/all_to_all | solution.py:34
  198.1 3.4 %convolution_convert_fusion = bf16[768,2,512]{2,0,1:T(8,128)(2,1)} fusion(bf16[2,512,512]{2,1,0:T(8,128)(2,1)} %param.15, bf16[256,512]{1,0:T(8,128)(2,1)S(1)} %bitcast.60, bf16[512,512]{1,0:T(8,128)(2,1)S(1)} %bitcast.53), kind=kOutput, calls=%fused_computation.4 | convolution fusion | flops 807665664 | bytes 3407872 | tf_op jit(solution)/shard_map/nf,sfh->nsh/dot_general | solution.py:11
  201.5 0.0 copy-start.2
  201.5 4.0 %gather_fusion.3 = bf16[24,128,512]{2,1,0:T(8,128)(2,1)} fusion(bf16[2,6,128,512]{3,2,1,0:T(8,128)(2,1)} %bitcast.56, s32[24]{0:T(128)S(1)} %reshape.95), kind=kCustom, calls=%fused_computation.3 | custom fusion | bytes 6291648 | tf_op jit(solution)/shard_map/vmap()/gather | solution.py:21
  205.4 0.0 copy-done.2
  205.4 0.0 copy-start.5
  205.4 2.5 %fusion.12 = f32[4,128,512,1,1]{2,1,4,0,3:T(8,128)S(1)} fusion(bf16[2,4,3,128,512]{4,3,2,1,0:T(8,128)(2,1)} %bitcast.54, bf16[2,4,3,128,128]{4,3,2,1,0:T(8,128)(2,1)S(1)} %copy-done.2, bf16[2,4,3]{2,1,0:T(4,128)(2,1)S(1)} %fusion.18), kind=kOutput, calls=%fused_computation.24 | convolution fusion | flops 403046400 | bytes 4980784 | tf_op jit(solution)/shard_map/sktab,sktbh->kah/dot_general | solution.py:28
  208.0 21.1 %all_to_all.35 = f32[32,16,512]{2,1,0:T(8,128)S(1)} all-to-all(f32[32,16,512]{2,1,0:T(8,128)S(1)} %bitcast.58), channel_id=1, replica_groups=mesh['rel'=8,'vrow'=32,'vcol'=4] {'rel','vcol'}, dimensions={0} | all-to-all | bytes 2097152 | tf_op jit(solution)/shard_map/all_to_all | solution.py:39
  229.0 0.1 reduce_sum.19
  229.1 0.0 copy-done.5
  229.1 1.8 fusion.9
  (3 shorter events, 0.0 us)
Async XLA Ops:
  0.0 102.3 %copy-start = (bf16[2,1024,512]{2,1,0:T(8,128)(2,1)S(1)}, bf16[2,1024,512]{2,1,0:T(8,128)(2,1)}, u32[]{:S(2)}) copy-start(bf16[2,1024,512]{2,1,0:T(8,128)(2,1)} %param.12) | copy-start | bytes 6291460
  2.8 35.2 %copy-start.3 = (s32[2,4,3]{1,0,2:T(2,128)S(1)}, s32[2,4,3]{1,0,2:T(2,128)}, u32[]{:S(2)}) copy-start(s32[2,4,3]{1,0,2:T(2,128)} %param.19) | copy-start | bytes 292
  2.8 35.4 %copy-start.6 = (s32[2,4,1]{1,2,0:T(1,128)S(1)}, s32[2,4,1]{1,2,0:T(1,128)}, u32[]{:S(2)}) copy-start(s32[2,4,1]{1,2,0:T(1,128)} %param.20) | copy-start | bytes 100
  2.8 99.5 %copy-start.1 = (bf16[512,1024]{1,0:T(8,128)(2,1)S(1)}, bf16[512,1024]{1,0:T(8,128)(2,1)}, u32[]{:S(2)}) copy-start(bf16[512,1024]{1,0:T(8,128)(2,1)} %param.11) | copy-start | bytes 3145732
  8.6 93.7 %all-to-all-start = ((bf16[32,8,1024]{2,1,0:T(8,128)(2,1)}), bf16[32,8,1024]{2,1,0:T(8,128)(2,1)}, u32[]{:S(2)}, u32[]{:S(2)}) async-start(bf16[32,8,1024]{2,1,0:T(8,128)(2,1)} %bitcast_select_fusion), calls=%async_computation | async-start | bytes 1048576 | tf_op jit(solution)/shard_map/all_to_all | solution.py:34
  110.2 24.8 %copy-start.4 = (f32[512]{0:T(512)S(1)}, f32[512]{0:T(512)}, u32[]{:S(2)}) copy-start(f32[512]{0:T(512)} %param.14) | copy-start | bytes 6148
  113.7 20.1 %all-to-all-start.1 = ((bf16[32,16,512]{2,1,0:T(8,128)(2,1)}), bf16[32,16,512]{2,1,0:T(8,128)(2,1)}, u32[]{:S(2)}, u32[]{:S(2)}) async-start(bf16[32,16,512]{2,1,0:T(8,128)(2,1)} %bitcast.59), calls=%async_computation.1 | async-start | bytes 1048576 | tf_op jit(solution)/shard_map/all_to_all | solution.py:39
  201.5 4.0 %copy-start.2 = (bf16[2,4,3,128,128]{4,3,2,1,0:T(8,128)(2,1)S(1)}, bf16[2,4,3,128,128]{4,3,2,1,0:T(8,128)(2,1)}, u32[]{:S(2)}) copy-start(bf16[2,4,3,128,128]{4,3,2,1,0:T(8,128)(2,1)} %param.18) | copy-start | bytes 2359300
  205.4 23.7 %copy-start.5 = (f32[512]{0:T(512)S(1)}, f32[512]{0:T(512)}, u32[]{:S(2)}) copy-start(f32[512]{0:T(512)} %param.17) | copy-start | bytes 6148

commit v2 on v1

--- a/solution.py
+++ b/solution.py
@@ -13,20 +13,27 @@
     )
 
 
-def gather_blocks(sources, tile_source, block_size):
+def gather_blocks(sources, picks, block_size):
     block_count = sources.shape[0] // block_size
     blocks = sources.reshape(block_count, block_size, sources.shape[1], sources.shape[2])
 
     def pick(source_blocks, indices):
         return source_blocks[indices]
 
-    return jax.vmap(pick, in_axes=(2, 0))(blocks, tile_source)
+    return jax.vmap(pick, in_axes=(2, 0))(blocks, picks)
 
 
-def aggregate(sources, masked, tile_source):
-    picked = gather_blocks(sources, tile_source, masked.shape[-1])
-    summed = jnp.einsum("sktab,sktbh->kah", masked, picked, preferred_element_type=jnp.float32)
+def aggregate(sources, weighted, picks):
+    picked = gather_blocks(sources, picks, weighted.shape[-1])
+    summed = jnp.einsum("sktab,sktbh->kah", weighted, picked, preferred_element_type=jnp.float32)
     return summed.reshape(-1, summed.shape[-1])
+
+
+def layer_part(own_rows, far_rows, weight, local_tiles, remote_tiles, local_pick, remote_pick):
+    own_proj = project(own_rows, weight)
+    own_sum = aggregate(own_proj, local_tiles, local_pick)
+    far_proj = project(far_rows, weight)
+    return own_sum + aggregate(far_proj, remote_tiles, remote_pick)
 
 
 def fetch_rows(values, send_index):
@@ -66,20 +73,24 @@
         tiles.dtype
     )
     masked = tiles * live_tiles[:, :, :, None, None]
+    local_rows_blocks = local_rows // tiles.shape[-1]
+    is_local = tile_source < local_rows_blocks
+    local_tiles = masked * is_local.astype(tiles.dtype)[:, :, :, None, None]
+    remote_tiles = masked * (~is_local).astype(tiles.dtype)[:, :, :, None, None]
+    local_pick = jnp.where(is_local, tile_source, 0)
+    remote_pick = jnp.where(is_local, 0, tile_source - local_rows_blocks)
     parts = lax.axis_size(GROUP)
     share_rows = local_rows // parts
     row_start = lax.axis_index(GROUP) * share_rows
     received = fetch_rows(features, send_index)
-    first_proj = project(jnp.concatenate([features, received], axis=0), first_weight)
-    first_part = aggregate(first_proj, masked, tile_source)
+    first_part = layer_part(features, received, first_weight, local_tiles, remote_tiles, local_pick, remote_pick)
     first_share = scatter_sum(first_part.astype(jnp.bfloat16), parts)
     own_features = lax.dynamic_slice_in_dim(features, row_start, share_rows, 0)
     first_term = jnp.dot(own_features, first_root, preferred_element_type=jnp.float32)
     hidden_share = jax.nn.relu(first_share + first_term + first_bias).astype(jnp.bfloat16)
     hidden = gather_all(hidden_share, parts)
     received_hidden = fetch_rows(hidden, send_index)
-    second_proj = project(jnp.concatenate([hidden, received_hidden], axis=0), second_weight)
-    second_part = aggregate(second_proj, masked, tile_source)
+    second_part = layer_part(hidden, received_hidden, second_weight, local_tiles, remote_tiles, local_pick, remote_pick)
     second_share = scatter_sum(second_part, parts)
     second_term = jnp.dot(hidden_share, second_root, preferred_element_type=jnp.float32)
     result = jax.nn.relu(second_share + second_term + second_bias).astype(jnp.bfloat16)

time: 232 us -> 230 us (level)
  blocking collectives: 81.4 us -> 36.6 us
  waiting for transfers between devices: 75.5 us -> 104 us
  local copies, waits for them, and re-layouts: 13.6 us -> 19.6 us
  starting transfers between devices: 38 us -> 42.5 us
  matrix products: 16.7 us -> 19.5 us
    all_to_all x1 -> x0, blocking collectives: 44.8 us -> none  [fetch_rows(): lax.all_to_all(outgoing, 'vrow', split_axis=0, concat_axis=0, tiled=True)]
    all_to_all x1 -> x2, waiting for transfers between devices: 64 us -> 92.9 us  [fetch_rows(): lax.all_to_all(outgoing, 'vrow', split_axis=0, concat_axis=0, tiled=True)]
    gather x4 -> x8, local copies, waits for them, and re-layouts: 8.02 us -> 12.8 us  [pick(): return source_blocks[indices]]
    all_to_all x1 -> x2, starting transfers between devices: 29.4 us -> 34 us  [fetch_rows(): lax.all_to_all(outgoing, 'vrow', split_axis=0, concat_axis=0, tiled=True)]
    dot_general x2 -> x4, matrix products: 6.09 us -> 7.53 us  [aggregate(): jnp.einsum('sktab,sktbh->kah', weighted, picked, preferred_element_type=j...]
    dot_general x2 -> x4, matrix products: 7.33 us -> 8.65 us  [project(): jnp.einsum('nf,sfh->nsh', row_values, weight, preferred_element_type=jnp....]
  transfers between devices with their start and end apart: 2 -> 3, of which waited for: 2 -> 3; matrix products, arithmetic and copies ran while one was open for 0% -> 6% of each run, Pallas kernels for 0% -> 0%
where the time goes in v2:
time: 230 us; the launch traced here: 229 us
  waiting for transfers between devices  104 us (45%)
  starting transfers between devices  42.5 us (18%)
  blocking collectives  36.6 us (16%)
  local copies, waits for them, and re-layouts  19.6 us (9%)
  matrix products  19.5 us (8%)
  other arithmetic  6.17 us (3%)
    all_to_all x2, waiting for transfers between devices, fetch_rows(): lax.all_to_all(outgoing, 'vrow', split_axis=0, concat_axis=0, tiled=True)  92.9 us
    all_to_all x2, starting transfers between devices, fetch_rows(): lax.all_to_all(outgoing, 'vrow', split_axis=0, concat_axis=0, tiled=True)  34 us
    all_to_all x1, blocking collectives, scatter_sum(): received = lax.all_to_all(chunks, GROUP, 0, 0, tiled=False)  21 us
    all_to_all x1, blocking collectives, gather_all(): received = lax.all_to_all(copies, GROUP, 0, 0, tiled=False)  15.5 us
    gather x8, local copies, waits for them, and re-layouts, pick(): return source_blocks[indices]  12.8 us
    all_to_all x1, waiting for transfers between devices, scatter_sum(): received = lax.all_to_all(chunks, GROUP, 0, 0, tiled=False)  11.4 us
    dot_general x4, matrix products, project(): jnp.einsum('nf,sfh->nsh', row_values, weight, preferred_element_type=jnp....  8.65 us
    all_to_all x1, starting transfers between devices, scatter_sum(): received = lax.all_to_all(chunks, GROUP, 0, 0, tiled=False)  8.55 us
  transfers between devices with their start and end apart: 3, of which 3 were waited for; matrix products, arithmetic and copies ran while one was open for 6% of the time, Pallas kernels for 0%

profile of v2, /device:TPU:1, one launch (start us, length us, event | category | flops | bytes accessed | tf_op | source)
XLA Modules:
  0.0 228.9 jit_solution(3132287587548440809)
XLA Ops:
  0.0 0.0 copy-start
  0.0 0.8 compare_select_fusion.3
  0.8 0.5 broadcast.149
  1.4 1.3 reduce.3
  2.7 0.1 reshape.92
  2.8 0.0 copy-start.5
  2.8 0.0 copy-start.1
  2.8 3.8 %gather_fusion = bf16[256,1024]{1,0:T(8,128)(2,1)} fusion(bf16[512,1024]{1,0:T(8,128)(2,1)} %param.11, s32[1024]{0:T(1024)S(1)} %pad_clamp_fusion), kind=kCustom, calls=%fused_computation | custom fusion | bytes 1049600 | tf_op jit(solution)/shard_map/jit(_take)/gather | solution.py:40
  6.6 2.0 bitcast_select_fusion
  8.6 29.4 %all-to-all-start = ((bf16[32,8,1024]{2,1,0:T(8,128)(2,1)}), bf16[32,8,1024]{2,1,0:T(8,128)(2,1)}, u32[]{:S(2)}, u32[]{:S(2)}) async-start(bf16[32,8,1024]{2,1,0:T(8,128)(2,1)} %bitcast_select_fusion), calls=%async_computation | async-start | bytes 1048576 | tf_op jit(solution)/shard_map/all_to_all | solution.py:41
  38.0 0.0 copy-done.5
  38.0 0.1 copy.25
  38.1 0.1 reshape.120
  38.2 0.1 copy.24
  38.4 0.1 copy.21
  38.5 0.1 reshape.114
  38.5 0.1 copy.20
  38.7 0.0 copy-done
  38.7 2.2 convolution_convert_fusion
  40.9 3.7 %gather_fusion.2 = bf16[24,128,512]{2,1,0:T(8,128)(2,1)} fusion(bf16[2,4,128,512]{3,2,1,0:T(8,128)(2,1)} %bitcast.99, s32[24]{0:T(128)S(1)} %reshape.114), kind=kCustom, calls=%fused_computation.2 | custom fusion | bytes 6291648 | tf_op jit(solution)/shard_map/vmap()/gather | solution.py:21
  44.6 0.1 fusion.30
  44.7 57.6 %all-to-all-done = bf16[32,8,1024]{2,1,0:T(8,128)(2,1)} async-done(((bf16[32,8,1024]{2,1,0:T(8,128)(2,1)}), bf16[32,8,1024]{2,1,0:T(8,128)(2,1)}, u32[]{:S(2)}, u32[]{:S(2)}) %all-to-all-start) | async-done | bytes 524320 | tf_op jit(solution)/shard_map/all_to_all | solution.py:41
  102.3 1.7 convolution_convert_fusion.3
  104.1 0.0 copy-start.4
  104.1 2.5 %gather_fusion.3 = bf16[24,128,512]{2,1,0:T(8,128)(2,1)} fusion(bf16[2,2,128,512]{3,2,1,0:T(8,128)(2,1)S(1)} %bitcast.91, s32[24]{0:T(128)S(1)} %reshape.120), kind=kCustom, calls=%fused_computation.3 | custom fusion | bytes 6291648 | tf_op jit(solution)/shard_map/vmap()/gather | solution.py:21
  106.6 2.7 %convolution_bitcast_fusion.2 = f32[4,128,512]{2,1,0:T(8,128)S(1)} fusion(bf16[2,4,3,128,512]{4,3,2,1,0:T(8,128)(2,1)} %bitcast.96, bf16[2,4,3,128,128]{4,3,2,1,0:T(8,128)(2,1)S(1)} %copy-done.4, bf16[2,4,3]{2,1,0:T(4,128)(2,1)S(1)} %copy.24, bf16[2,4,3]{2,1,0:T(4,128)(2,1)S(1)} %fusion.30), kind=kOutput, calls=%fused_computation.10 | convolution fusion | flops 403439616 | bytes 4980832 | tf_op jit(solution)/shard_map/sktab,sktbh->kah/dot_general | solution.py:28
  109.3 0.1 copy-done.3
  109.4 1.5 fusion.2
  110.9 8.6 %all-to-all-start.1 = ((bf16[32,16,512]{2,1,0:T(8,128)(2,1)}), bf16[32,16,512]{2,1,0:T(8,128)(2,1)S(1)}, u32[]{:S(2)}, u32[]{:S(2)}) async-start(bf16[32,16,512]{2,1,0:T(8,128)(2,1)} %bitcast.101), calls=%async_computation.1 | async-start | bytes 1048576 | tf_op jit(solution)/shard_map/all_to_all | solution.py:46
  119.5 11.4 %all-to-all-done.1 = bf16[32,16,512]{2,1,0:T(8,128)(2,1)S(1)} async-done(((bf16[32,16,512]{2,1,0:T(8,128)(2,1)}), bf16[32,16,512]{2,1,0:T(8,128)(2,1)S(1)}, u32[]{:S(2)}, u32[]{:S(2)}) %all-to-all-start.1) | async-done | bytes 524320 | tf_op jit(solution)/shard_map/all_to_all | solution.py:46
  130.9 0.1 convert_reduce_fusion
  131.0 1.5 fusion.8
  132.5 0.1 broadcast_in_dim.54
  132.6 15.5 %all_to_all.33 = bf16[32,16,512]{2,1,0:T(8,128)(2,1)S(1)} all-to-all(bf16[32,16,512]{2,1,0:T(8,128)(2,1)S(1)} %broadcast_in_dim.54), channel_id=1, replica_groups=mesh['rel'=8,'vrow'=32,'vcol'=4] {'rel','vcol'}, dimensions={0} | all-to-all | bytes 1048576 | tf_op jit(solution)/shard_map/all_to_all | solution.py:52
  148.1 1.8 gather_fusion.1
  149.9 1.8 bitcast_select_fusion.1
  151.7 4.6 %all-to-all-start.3 = ((bf16[32,8,512]{2,1,0:T(8,128)(2,1)}), bf16[32,8,512]{2,1,0:T(8,128)(2,1)}, u32[]{:S(2)}, u32[]{:S(2)}) async-start(bf16[32,8,512]{2,1,0:T(8,128)(2,1)} %bitcast_select_fusion.1), calls=%async_computation.3 | async-start | bytes 524288 | tf_op jit(solution)/shard_map/all_to_all | solution.py:41
  156.3 2.9 %convolution_convert_fusion.1 = bf16[512,2,512]{2,0,1:T(8,128)(2,1)} fusion(bf16[512,512,1]{1,0,2:T(8,128)(2,1)S(1)} %bitcast.93, bf16[2,512,512]{2,1,0:T(8,128)(2,1)} %param.15), kind=kOutput, calls=%fused_computation.7 | convolution fusion | flops 537395200 | bytes 2621440 | tf_op jit(solution)/shard_map/nf,sfh->nsh/dot_general | solution.py:11
  159.2 3.7 %gather_fusion.4 = bf16[24,128,512]{2,1,0:T(8,128)(2,1)} fusion(bf16[2,4,128,512]{3,2,1,0:T(8,128)(2,1)} %bitcast.98, s32[24]{0:T(128)S(1)} %reshape.114), kind=kCustom, calls=%fused_computation.4 | custom fusion | bytes 6291648 | tf_op jit(solution)/shard_map/vmap()/gather | solution.py:21
  162.9 35.2 %all-to-all-done.3 = bf16[32,8,512]{2,1,0:T(8,128)(2,1)} async-done(((bf16[32,8,512]{2,1,0:T(8,128)(2,1)}), bf16[32,8,512]{2,1,0:T(8,128)(2,1)}, u32[]{:S(2)}, u32[]{:S(2)}) %all-to-all-start.3) | async-done | bytes 262176 | tf_op jit(solution)/shard_map/all_to_all | solution.py:41
  198.1 1.7 convolution_convert_fusion.2
  199.9 2.5 %gather_fusion.5 = bf16[24,128,512]{2,1,0:T(8,128)(2,1)} fusion(bf16[2,2,128,512]{3,2,1,0:T(8,128)(2,1)S(1)} %bitcast.90, s32[24]{0:T(128)S(1)} %reshape.120), kind=kCustom, calls=%fused_computation.5 | custom fusion | bytes 6291648 | tf_op jit(solution)/shard_map/vmap()/gather | solution.py:21
  202.4 2.7 %convolution_bitcast_fusion = f32[4,128,512]{2,1,0:T(8,128)S(1)} fusion(bf16[2,4,3,128,512]{4,3,2,1,0:T(8,128)(2,1)} %bitcast.95, bf16[2,4,3,128,128]{4,3,2,1,0:T(8,128)(2,1)S(1)} %copy-done.4, bf16[2,4,3]{2,1,0:T(4,128)(2,1)S(1)} %copy.24, bf16[2,4,3]{2,1,0:T(4,128)(2,1)S(1)} %fusion.30), kind=kOutput, calls=%fused_computation.8 | convolution fusion | flops 403439616 | bytes 4980832 | tf_op jit(solution)/shard_map/sktab,sktbh->kah/dot_general | solution.py:28
  205.1 0.1 copy-done.2
  205.2 0.7 fusion.1
  205.9 21.0 %all_to_all.34 = f32[32,16,512]{2,1,0:T(8,128)S(1)} all-to-all(f32[32,16,512]{2,1,0:T(8,128)S(1)} %bitcast.100), channel_id=1, replica_groups=mesh['rel'=8,'vrow'=32,'vcol'=4] {'rel','vcol'}, dimensions={0} | all-to-all | bytes 2097152 | tf_op jit(solution)/shard_map/all_to_all | solution.py:46
  226.9 0.1 reduce_sum.19
  227.0 1.8 fusion.9
  (14 shorter events, 0.1 us)
Async XLA Ops:
  0.0 38.7 %copy-start = (bf16[2,1024,512]{2,1,0:T(8,128)(2,1)S(1)}, bf16[2,1024,512]{2,1,0:T(8,128)(2,1)}, u32[]{:S(2)}) copy-start(bf16[2,1024,512]{2,1,0:T(8,128)(2,1)} %param.12) | copy-start | bytes 6291460
  2.8 35.2 %copy-start.5 = (s32[2,4,3]{1,0,2:T(2,128)S(1)}, s32[2,4,3]{1,0,2:T(2,128)}, u32[]{:S(2)}) copy-start(s32[2,4,3]{1,0,2:T(2,128)} %param.19) | copy-start | bytes 292
  2.8 35.8 %copy-start.1 = (bf16[512,1024]{1,0:T(8,128)(2,1)S(1)}, bf16[512,1024]{1,0:T(8,128)(2,1)}, u32[]{:S(2)}) copy-start(bf16[512,1024]{1,0:T(8,128)(2,1)} %param.11) | copy-start | bytes 3145732
  8.6 93.7 %all-to-all-start = ((bf16[32,8,1024]{2,1,0:T(8,128)(2,1)}), bf16[32,8,1024]{2,1,0:T(8,128)(2,1)}, u32[]{:S(2)}, u32[]{:S(2)}) async-start(bf16[32,8,1024]{2,1,0:T(8,128)(2,1)} %bitcast_select_fusion), calls=%async_computation | async-start | bytes 1048576 | tf_op jit(solution)/shard_map/all_to_all | solution.py:41
  40.9 3.7 %copy-start.8 = (s32[2,4,1]{1,2,0:T(1,128)S(1)}, s32[2,4,1]{1,2,0:T(1,128)}, u32[]{:S(2)}) copy-start(s32[2,4,1]{1,2,0:T(1,128)} %param.20) | copy-start | bytes 100
  104.1 2.5 %copy-start.4 = (bf16[2,4,3,128,128]{4,3,2,1,0:T(8,128)(2,1)S(1)}, bf16[2,4,3,128,128]{4,3,2,1,0:T(8,128)(2,1)}, u32[]{:S(2)}) copy-start(bf16[2,4,3,128,128]{4,3,2,1,0:T(8,128)(2,1)} %param.18) | copy-start | bytes 2359300
  106.6 2.8 %copy-start.3 = (bf16[24,128,512]{2,1,0:T(8,128)(2,1)S(1)}, bf16[24,128,512]{2,1,0:T(8,128)(2,1)}, u32[]{:S(2)}) copy-start(bf16[24,128,512]{2,1,0:T(8,128)(2,1)} %gather_fusion.2) | copy-start | bytes 9437188
  109.4 21.6 %copy-start.6 = (f32[512]{0:T(512)S(1)}, f32[512]{0:T(512)}, u32[]{:S(2)}) copy-start(f32[512]{0:T(512)} %param.14) | copy-start | bytes 6148
  110.9 20.0 %all-to-all-start.1 = ((bf16[32,16,512]{2,1,0:T(8,128)(2,1)}), bf16[32,16,512]{2,1,0:T(8,128)(2,1)S(1)}, u32[]{:S(2)}, u32[]{:S(2)}) async-start(bf16[32,16,512]{2,1,0:T(8,128)(2,1)} %bitcast.101), calls=%async_computation.1 | async-start | bytes 1048576 | tf_op jit(solution)/shard_map/all_to_all | solution.py:46
  151.7 46.4 %all-to-all-start.3 = ((bf16[32,8,512]{2,1,0:T(8,128)(2,1)}), bf16[32,8,512]{2,1,0:T(8,128)(2,1)}, u32[]{:S(2)}, u32[]{:S(2)}) async-start(bf16[32,8,512]{2,1,0:T(8,128)(2,1)} %bitcast_select_fusion.1), calls=%async_computation.3 | async-start | bytes 524288 | tf_op jit(solution)/shard_map/all_to_all | solution.py:41
  202.4 2.8 %copy-start.2 = (bf16[24,128,512]{2,1,0:T(8,128)(2,1)S(1)}, bf16[24,128,512]{2,1,0:T(8,128)(2,1)}, u32[]{:S(2)}) copy-start(bf16[24,128,512]{2,1,0:T(8,128)(2,1)} %gather_fusion.4) | copy-start | bytes 9437188
  205.2 21.8 %copy-start.7 = (f32[512]{0:T(512)S(1)}, f32[512]{0:T(512)}, u32[]{:S(2)}) copy-start(f32[512]{0:T(512)} %param.17) | copy-start | bytes 6148

commit v3 on v2

--- a/solution.py
+++ b/solution.py
@@ -91,7 +91,7 @@
     hidden = gather_all(hidden_share, parts)
     received_hidden = fetch_rows(hidden, send_index)
     second_part = layer_part(hidden, received_hidden, second_weight, local_tiles, remote_tiles, local_pick, remote_pick)
-    second_share = scatter_sum(second_part, parts)
+    second_share = scatter_sum(second_part.astype(jnp.bfloat16), parts)
     second_term = jnp.dot(hidden_share, second_root, preferred_element_type=jnp.float32)
     result = jax.nn.relu(second_share + second_term + second_bias).astype(jnp.bfloat16)
     return result[None]

time: 230 us -> 224 us (0.974)
  blocking collectives: 36.6 us -> 32 us
    all_to_all x1, blocking collectives: 21 us -> 16.5 us  [scatter_sum(): received = lax.all_to_all(chunks, GROUP, 0, 0, tiled=False)]
where the time goes in v3:
time: 224 us; the launch traced here: 223 us
  waiting for transfers between devices  104 us (46%)
  starting transfers between devices  42.5 us (19%)
  blocking collectives  32 us (14%)
  local copies, waits for them, and re-layouts  19.6 us (9%)
  matrix products  18.5 us (8%)
  other arithmetic  6.17 us (3%)
    all_to_all x2, waiting for transfers between devices, fetch_rows(): lax.all_to_all(outgoing, 'vrow', split_axis=0, concat_axis=0, tiled=True)  92.8 us
    all_to_all x2, starting transfers between devices, fetch_rows(): lax.all_to_all(outgoing, 'vrow', split_axis=0, concat_axis=0, tiled=True)  34 us
    all_to_all x1, blocking collectives, scatter_sum(): received = lax.all_to_all(chunks, GROUP, 0, 0, tiled=False)  16.5 us
    all_to_all x1, blocking collectives, gather_all(): received = lax.all_to_all(copies, GROUP, 0, 0, tiled=False)  15.5 us
    gather x8, local copies, waits for them, and re-layouts, pick(): return source_blocks[indices]  12.8 us
    all_to_all x1, waiting for transfers between devices, scatter_sum(): received = lax.all_to_all(chunks, GROUP, 0, 0, tiled=False)  11.4 us
    dot_general x4, matrix products, project(): jnp.einsum('nf,sfh->nsh', row_values, weight, preferred_element_type=jnp....  8.67 us
    all_to_all x1, starting transfers between devices, scatter_sum(): received = lax.all_to_all(chunks, GROUP, 0, 0, tiled=False)  8.56 us
  transfers between devices with their start and end apart: 3, of which 3 were waited for; matrix products, arithmetic and copies ran while one was open for 6% of the time, Pallas kernels for 0%

profile of v3, /device:TPU:1, one launch (start us, length us, event | category | flops | bytes accessed | tf_op | source)
XLA Modules:
  0.0 223.3 jit_solution(12250467095589427904)
XLA Ops:
  0.0 0.0 copy-start
  0.0 0.8 compare_select_fusion.3
  0.8 0.5 broadcast.149
  1.4 1.3 reduce.3
  2.7 0.1 reshape.93
  2.8 0.0 copy-start.6
  2.8 0.0 copy-start.1
  2.8 3.8 %gather_fusion = bf16[256,1024]{1,0:T(8,128)(2,1)} fusion(bf16[512,1024]{1,0:T(8,128)(2,1)} %param.11, s32[1024]{0:T(1024)S(1)} %pad_clamp_fusion), kind=kCustom, calls=%fused_computation | custom fusion | bytes 1049600 | tf_op jit(solution)/shard_map/jit(_take)/gather | solution.py:40
  6.6 2.0 bitcast_select_fusion
  8.6 29.4 %all-to-all-start = ((bf16[32,8,1024]{2,1,0:T(8,128)(2,1)}), bf16[32,8,1024]{2,1,0:T(8,128)(2,1)}, u32[]{:S(2)}, u32[]{:S(2)}) async-start(bf16[32,8,1024]{2,1,0:T(8,128)(2,1)} %bitcast_select_fusion), calls=%async_computation | async-start | bytes 1048576 | tf_op jit(solution)/shard_map/all_to_all | solution.py:41
  38.0 0.0 copy-done.6
  38.0 0.1 copy.25
  38.1 0.1 reshape.121
  38.2 0.1 copy.24
  38.3 0.1 copy.21
  38.4 0.1 reshape.115
  38.5 0.1 copy.20
  38.6 0.0 copy-done
  38.6 2.3 %convolution_convert_fusion = bf16[512,2,512]{2,0,1:T(8,128)(2,1)} fusion(bf16[2,1024,512]{2,1,0:T(8,128)(2,1)S(1)} %copy-done, bf16[512,1024]{1,0:T(8,128)(2,1)S(1)} %copy-done.1), kind=kOutput, calls=%fused_computation.6 | convolution fusion | flops 1074266112 | bytes 4194304 | tf_op jit(solution)/shard_map/nf,sfh->nsh/dot_general | solution.py:11
  40.9 3.7 %gather_fusion.2 = bf16[24,128,512]{2,1,0:T(8,128)(2,1)} fusion(bf16[2,4,128,512]{3,2,1,0:T(8,128)(2,1)} %bitcast.101, s32[24]{0:T(128)S(1)} %reshape.115), kind=kCustom, calls=%fused_computation.2 | custom fusion | bytes 6291648 | tf_op jit(solution)/shard_map/vmap()/gather | solution.py:21
  44.6 0.1 fusion.31
  44.7 57.6 %all-to-all-done = bf16[32,8,1024]{2,1,0:T(8,128)(2,1)} async-done(((bf16[32,8,1024]{2,1,0:T(8,128)(2,1)}), bf16[32,8,1024]{2,1,0:T(8,128)(2,1)}, u32[]{:S(2)}, u32[]{:S(2)}) %all-to-all-start) | async-done | bytes 524320 | tf_op jit(solution)/shard_map/all_to_all | solution.py:41
  102.3 1.7 convolution_convert_fusion.3
  104.1 0.0 copy-start.4
  104.1 2.5 %gather_fusion.3 = bf16[24,128,512]{2,1,0:T(8,128)(2,1)} fusion(bf16[2,2,128,512]{3,2,1,0:T(8,128)(2,1)S(1)} %bitcast.93, s32[24]{0:T(128)S(1)} %reshape.121), kind=kCustom, calls=%fused_computation.3 | custom fusion | bytes 6291648 | tf_op jit(solution)/shard_map/vmap()/gather | solution.py:21
  106.6 2.7 %convolution_bitcast_fusion.2 = f32[4,128,512]{2,1,0:T(8,128)S(1)} fusion(bf16[2,4,3,128,512]{4,3,2,1,0:T(8,128)(2,1)} %bitcast.97, bf16[2,4,3,128,128]{4,3,2,1,0:T(8,128)(2,1)S(1)} %copy-done.4, bf16[2,4,3]{2,1,0:T(4,128)(2,1)S(1)} %copy.24, bf16[2,4,3]{2,1,0:T(4,128)(2,1)S(1)} %fusion.31), kind=kOutput, calls=%fused_computation.10 | convolution fusion | flops 403439616 | bytes 4980832 | tf_op jit(solution)/shard_map/sktab,sktbh->kah/dot_general | solution.py:28
  109.3 0.1 copy-done.3
  109.4 1.5 fusion.3
  110.9 8.6 %all-to-all-start.1 = ((bf16[32,16,512]{2,1,0:T(8,128)(2,1)}), bf16[32,16,512]{2,1,0:T(8,128)(2,1)S(1)}, u32[]{:S(2)}, u32[]{:S(2)}) async-start(bf16[32,16,512]{2,1,0:T(8,128)(2,1)} %bitcast.102), calls=%async_computation.1 | async-start | bytes 1048576 | tf_op jit(solution)/shard_map/all_to_all | solution.py:46
  119.5 11.4 %all-to-all-done.1 = bf16[32,16,512]{2,1,0:T(8,128)(2,1)S(1)} async-done(((bf16[32,16,512]{2,1,0:T(8,128)(2,1)}), bf16[32,16,512]{2,1,0:T(8,128)(2,1)S(1)}, u32[]{:S(2)}, u32[]{:S(2)}) %all-to-all-start.1) | async-done | bytes 524320 | tf_op jit(solution)/shard_map/all_to_all | solution.py:46
  130.9 0.1 convert_reduce_fusion.1
  131.0 1.5 fusion.9
  132.5 0.1 broadcast_in_dim.54
  132.6 15.5 %all_to_all.33 = bf16[32,16,512]{2,1,0:T(8,128)(2,1)S(1)} all-to-all(bf16[32,16,512]{2,1,0:T(8,128)(2,1)S(1)} %broadcast_in_dim.54), channel_id=1, replica_groups=mesh['rel'=8,'vrow'=32,'vcol'=4] {'rel','vcol'}, dimensions={0} | all-to-all | bytes 1048576 | tf_op jit(solution)/shard_map/all_to_all | solution.py:52
  148.1 1.8 gather_fusion.1
  149.9 1.7 bitcast_select_fusion.1
  151.7 4.6 %all-to-all-start.3 = ((bf16[32,8,512]{2,1,0:T(8,128)(2,1)}), bf16[32,8,512]{2,1,0:T(8,128)(2,1)}, u32[]{:S(2)}, u32[]{:S(2)}) async-start(bf16[32,8,512]{2,1,0:T(8,128)(2,1)} %bitcast_select_fusion.1), calls=%async_computation.3 | async-start | bytes 524288 | tf_op jit(solution)/shard_map/all_to_all | solution.py:41
  156.3 2.9 %convolution_convert_fusion.1 = bf16[512,2,512]{2,0,1:T(8,128)(2,1)} fusion(bf16[512,512,1]{1,0,2:T(8,128)(2,1)S(1)} %bitcast.95, bf16[2,512,512]{2,1,0:T(8,128)(2,1)} %param.15), kind=kOutput, calls=%fused_computation.7 | convolution fusion | flops 537395200 | bytes 2621440 | tf_op jit(solution)/shard_map/nf,sfh->nsh/dot_general | solution.py:11
  159.2 3.7 %gather_fusion.4 = bf16[24,128,512]{2,1,0:T(8,128)(2,1)} fusion(bf16[2,4,128,512]{3,2,1,0:T(8,128)(2,1)} %bitcast.100, s32[24]{0:T(128)S(1)} %reshape.115), kind=kCustom, calls=%fused_computation.4 | custom fusion | bytes 6291648 | tf_op jit(solution)/shard_map/vmap()/gather | solution.py:21
  162.9 35.2 %all-to-all-done.3 = bf16[32,8,512]{2,1,0:T(8,128)(2,1)} async-done(((bf16[32,8,512]{2,1,0:T(8,128)(2,1)}), bf16[32,8,512]{2,1,0:T(8,128)(2,1)}, u32[]{:S(2)}, u32[]{:S(2)}) %all-to-all-start.3) | async-done | bytes 262176 | tf_op jit(solution)/shard_map/all_to_all | solution.py:41
  198.1 1.7 convolution_convert_fusion.2
  199.9 2.5 %gather_fusion.5 = bf16[24,128,512]{2,1,0:T(8,128)(2,1)} fusion(bf16[2,2,128,512]{3,2,1,0:T(8,128)(2,1)S(1)} %bitcast.92, s32[24]{0:T(128)S(1)} %reshape.121), kind=kCustom, calls=%fused_computation.5 | custom fusion | bytes 6291648 | tf_op jit(solution)/shard_map/vmap()/gather | solution.py:21
  202.4 2.7 %convolution_bitcast_fusion = f32[4,128,512]{2,1,0:T(8,128)S(1)} fusion(bf16[2,4,3,128,512]{4,3,2,1,0:T(8,128)(2,1)} %bitcast.96, bf16[2,4,3,128,128]{4,3,2,1,0:T(8,128)(2,1)S(1)} %copy-done.4, bf16[2,4,3]{2,1,0:T(4,128)(2,1)S(1)} %copy.24, bf16[2,4,3]{2,1,0:T(4,128)(2,1)S(1)} %fusion.31), kind=kOutput, calls=%fused_computation.8 | convolution fusion | flops 403439616 | bytes 4980832 | tf_op jit(solution)/shard_map/sktab,sktbh->kah/dot_general | solution.py:28
  205.1 0.1 copy-done.2
  205.2 0.7 fusion.2
  205.9 16.5 %all_to_all.34 = bf16[32,16,512]{2,1,0:T(8,128)(2,1)S(1)} all-to-all(bf16[32,16,512]{2,1,0:T(8,128)(2,1)S(1)} %bitcast.103), channel_id=1, replica_groups=mesh['rel'=8,'vrow'=32,'vcol'=4] {'rel','vcol'}, dimensions={0} | all-to-all | bytes 1048576 | tf_op jit(solution)/shard_map/all_to_all | solution.py:46
  222.4 0.1 convert_reduce_fusion
  222.5 0.8 fusion.10
  (16 shorter events, 0.1 us)
Async XLA Ops:
  0.0 38.6 %copy-start = (bf16[2,1024,512]{2,1,0:T(8,128)(2,1)S(1)}, bf16[2,1024,512]{2,1,0:T(8,128)(2,1)}, u32[]{:S(2)}) copy-start(bf16[2,1024,512]{2,1,0:T(8,128)(2,1)} %param.12) | copy-start | bytes 6291460
  2.8 35.2 %copy-start.6 = (s32[2,4,3]{1,0,2:T(2,128)S(1)}, s32[2,4,3]{1,0,2:T(2,128)}, u32[]{:S(2)}) copy-start(s32[2,4,3]{1,0,2:T(2,128)} %param.19) | copy-start | bytes 292
  2.8 35.8 %copy-start.1 = (bf16[512,1024]{1,0:T(8,128)(2,1)S(1)}, bf16[512,1024]{1,0:T(8,128)(2,1)}, u32[]{:S(2)}) copy-start(bf16[512,1024]{1,0:T(8,128)(2,1)} %param.11) | copy-start | bytes 3145732
  8.6 93.7 %all-to-all-start = ((bf16[32,8,1024]{2,1,0:T(8,128)(2,1)}), bf16[32,8,1024]{2,1,0:T(8,128)(2,1)}, u32[]{:S(2)}, u32[]{:S(2)}) async-start(bf16[32,8,1024]{2,1,0:T(8,128)(2,1)} %bitcast_select_fusion), calls=%async_computation | async-start | bytes 1048576 | tf_op jit(solution)/shard_map/all_to_all | solution.py:41
  40.9 3.7 %copy-start.9 = (s32[2,4,1]{1,2,0:T(1,128)S(1)}, s32[2,4,1]{1,2,0:T(1,128)}, u32[]{:S(2)}) copy-start(s32[2,4,1]{1,2,0:T(1,128)} %param.20) | copy-start | bytes 100
  104.1 2.5 %copy-start.4 = (bf16[2,4,3,128,128]{4,3,2,1,0:T(8,128)(2,1)S(1)}, bf16[2,4,3,128,128]{4,3,2,1,0:T(8,128)(2,1)}, u32[]{:S(2)}) copy-start(bf16[2,4,3,128,128]{4,3,2,1,0:T(8,128)(2,1)} %param.18) | copy-start | bytes 2359300
  106.6 2.8 %copy-start.3 = (bf16[24,128,512]{2,1,0:T(8,128)(2,1)S(1)}, bf16[24,128,512]{2,1,0:T(8,128)(2,1)}, u32[]{:S(2)}) copy-start(bf16[24,128,512]{2,1,0:T(8,128)(2,1)} %gather_fusion.2) | copy-start | bytes 9437188
  109.4 21.6 %copy-start.7 = (f32[512]{0:T(512)S(1)}, f32[512]{0:T(512)}, u32[]{:S(2)}) copy-start(f32[512]{0:T(512)} %param.14) | copy-start | bytes 6148
  110.9 20.0 %all-to-all-start.1 = ((bf16[32,16,512]{2,1,0:T(8,128)(2,1)}), bf16[32,16,512]{2,1,0:T(8,128)(2,1)S(1)}, u32[]{:S(2)}, u32[]{:S(2)}) async-start(bf16[32,16,512]{2,1,0:T(8,128)(2,1)} %bitcast.102), calls=%async_computation.1 | async-start | bytes 1048576 | tf_op jit(solution)/shard_map/all_to_all | solution.py:46
  151.7 46.4 %all-to-all-start.3 = ((bf16[32,8,512]{2,1,0:T(8,128)(2,1)}), bf16[32,8,512]{2,1,0:T(8,128)(2,1)}, u32[]{:S(2)}, u32[]{:S(2)}) async-start(bf16[32,8,512]{2,1,0:T(8,128)(2,1)} %bitcast_select_fusion.1), calls=%async_computation.3 | async-start | bytes 524288 | tf_op jit(solution)/shard_map/all_to_all | solution.py:41
  202.4 2.8 %copy-start.2 = (bf16[24,128,512]{2,1,0:T(8,128)(2,1)S(1)}, bf16[24,128,512]{2,1,0:T(8,128)(2,1)}, u32[]{:S(2)}) copy-start(bf16[24,128,512]{2,1,0:T(8,128)(2,1)} %gather_fusion.4) | copy-start | bytes 9437188
  205.2 17.2 %copy-start.5 = (bf16[512,512]{1,0:T(8,128)(2,1)S(1)}, bf16[512,512]{1,0:T(8,128)(2,1)}, u32[]{:S(2)}) copy-start(bf16[512,512]{1,0:T(8,128)(2,1)} %param.16) | copy-start | bytes 1572868
  205.2 17.3 %copy-start.8 = (f32[512]{0:T(512)S(1)}, f32[512]{0:T(512)}, u32[]{:S(2)}) copy-start(f32[512]{0:T(512)} %param.17) | copy-start | bytes 6148

commit v4 on v3

--- a/solution.py
+++ b/solution.py
@@ -37,7 +37,8 @@
 
 
 def fetch_rows(values, send_index):
-    outgoing = jnp.take(values, send_index, axis=0)
+    chooser = (send_index[:, None] == jnp.arange(values.shape[0], dtype=send_index.dtype)[None, :])
+    outgoing = jnp.dot(chooser.astype(values.dtype), values, preferred_element_type=jnp.float32).astype(values.dtype)
     return lax.all_to_all(outgoing, "vrow", split_axis=0, concat_axis=0, tiled=True)
 
 

time: 224 us -> 216 us (0.964)
  local copies, waits for them, and re-layouts: 19.6 us -> 12.1 us
  other arithmetic: 6.17 us -> 1.64 us
  matrix products: 18.5 us -> 22.5 us
    gather x2 -> x0, local copies, waits for them, and re-layouts: 5.65 us -> none  [fetch_rows(): outgoing = jnp.take(values, send_index, axis=0)]
    select_n x3 -> x0, other arithmetic: 4.55 us -> none  [fetch_rows(): outgoing = jnp.take(values, send_index, axis=0)]
    dot_general x0 -> x2, matrix products: none -> 3.73 us  [fetch_rows(): jnp.dot(chooser.astype(values.dtype), values, preferred_element_type=jnp....]
where the time goes in v4:
time: 216 us; the launch traced here: 215 us
  waiting for transfers between devices  104 us (48%)
  starting transfers between devices  42.7 us (20%)
  blocking collectives  32 us (15%)
  matrix products  22.5 us (10%)
  local copies, waits for them, and re-layouts  12.1 us (6%)
    all_to_all x2, waiting for transfers between devices, fetch_rows(): lax.all_to_all(outgoing, 'vrow', split_axis=0, concat_axis=0, tiled=True)  92.5 us
    all_to_all x2, starting transfers between devices, fetch_rows(): lax.all_to_all(outgoing, 'vrow', split_axis=0, concat_axis=0, tiled=True)  34 us
    all_to_all x1, blocking collectives, scatter_sum(): received = lax.all_to_all(chunks, GROUP, 0, 0, tiled=False)  16.5 us
    all_to_all x1, blocking collectives, gather_all(): received = lax.all_to_all(copies, GROUP, 0, 0, tiled=False)  15.5 us
    gather x8, local copies, waits for them, and re-layouts, pick(): return source_blocks[indices]  11.5 us
    all_to_all x1, waiting for transfers between devices, scatter_sum(): received = lax.all_to_all(chunks, GROUP, 0, 0, tiled=False)  11.4 us
    dot_general x4, matrix products, project(): jnp.einsum('nf,sfh->nsh', row_values, weight, preferred_element_type=jnp....  8.9 us
    all_to_all x1, starting transfers between devices, scatter_sum(): received = lax.all_to_all(chunks, GROUP, 0, 0, tiled=False)  8.68 us
  transfers between devices with their start and end apart: 3, of which 3 were waited for; matrix products, arithmetic and copies ran while one was open for 6% of the time, Pallas kernels for 0%

profile of v4, /device:TPU:1, one launch (start us, length us, event | category | flops | bytes accessed | tf_op | source)
XLA Modules:
  0.0 214.9 jit_solution(426837593306179953)
XLA Ops:
  0.0 0.0 copy-start
  0.0 2.7 %fusion.4 = bf16[32,8,1024]{2,1,0:T(8,128)(2,1)} fusion(bf16[512,1024]{1,0:T(8,128)(2,1)} %param.11, s32[256]{0:T(256)} %bitcast.104), kind=kOutput, calls=%fused_computation.17 | convolution fusion | flops 268828672 | bytes 1573888 | tf_op jit(solution)/shard_map/dot_general | solution.py:41
  2.7 29.4 %all-to-all-start = ((bf16[32,8,1024]{2,1,0:T(8,128)(2,1)}), bf16[32,8,1024]{2,1,0:T(8,128)(2,1)}, u32[]{:S(2)}, u32[]{:S(2)}) async-start(bf16[32,8,1024]{2,1,0:T(8,128)(2,1)} %fusion.4), calls=%async_computation | async-start | bytes 1048576 | tf_op jit(solution)/shard_map/all_to_all | solution.py:42
  32.1 0.7 fusion.39
  32.8 0.1 copy.25
  32.9 0.1 reshape.54
  33.0 0.7 fusion.44
  33.7 0.1 copy.24
  33.8 0.1 copy.21
  33.9 0.1 reshape.48
  34.0 0.1 copy.20
  34.1 0.0 copy-done
  34.1 2.5 %convolution_convert_fusion = bf16[512,2,512]{2,0,1:T(8,128)(2,1)S(1)} fusion(bf16[2,1024,512]{2,1,0:T(8,128)(2,1)S(1)} %copy-done, bf16[512,1024]{1,0:T(8,128)(2,1)} %param.11), kind=kOutput, calls=%fused_computation.4 | convolution fusion | flops 1074266112 | bytes 4194304 | tf_op jit(solution)/shard_map/nf,sfh->nsh/dot_general | solution.py:11
  36.6 0.0 copy-start.8
  36.6 2.4 %gather_fusion = bf16[24,128,512]{2,1,0:T(8,128)(2,1)} fusion(bf16[2,4,128,512]{3,2,1,0:T(8,128)(2,1)S(1)} %bitcast.99, s32[24]{0:T(128)S(1)} %reshape.48), kind=kCustom, calls=%fused_computation | custom fusion | bytes 6291648 | tf_op jit(solution)/shard_map/vmap()/gather | solution.py:21
  39.0 0.0 copy-done.8
  39.0 0.1 fusion.35
  39.1 57.3 %all-to-all-done = bf16[32,8,1024]{2,1,0:T(8,128)(2,1)} async-done(((bf16[32,8,1024]{2,1,0:T(8,128)(2,1)}), bf16[32,8,1024]{2,1,0:T(8,128)(2,1)}, u32[]{:S(2)}, u32[]{:S(2)}) %all-to-all-start) | async-done | bytes 524320 | tf_op jit(solution)/shard_map/all_to_all | solution.py:42
  96.4 1.7 convolution_convert_fusion.4
  98.1 0.0 copy-start.3
  98.2 2.5 %gather_fusion.1 = bf16[24,128,512]{2,1,0:T(8,128)(2,1)} fusion(bf16[2,2,128,512]{3,2,1,0:T(8,128)(2,1)S(1)} %bitcast.93, s32[24]{0:T(128)S(1)} %reshape.54), kind=kCustom, calls=%fused_computation.1 | custom fusion | bytes 6291648 | tf_op jit(solution)/shard_map/vmap()/gather | solution.py:21
  100.7 0.0 copy-done.3
  100.7 2.7 %convolution_bitcast_fusion.2 = f32[4,128,512]{2,1,0:T(8,128)S(1)} fusion(bf16[2,4,3,128,512]{4,3,2,1,0:T(8,128)(2,1)} %bitcast.95, bf16[2,4,3,128,128]{4,3,2,1,0:T(8,128)(2,1)S(1)} %copy-done.3, bf16[2,4,3]{2,1,0:T(4,128)(2,1)S(1)} %copy.24, bf16[2,4,3]{2,1,0:T(4,128)(2,1)S(1)} %fusion.35), kind=kOutput, calls=%fused_computation.8 | convolution fusion | flops 403439616 | bytes 4980832 | tf_op jit(solution)/shard_map/sktab,sktbh->kah/dot_general | solution.py:28
  103.3 0.1 copy-done.2
  103.5 1.5 fusion.3
  105.0 8.7 %all-to-all-start.1 = ((bf16[32,16,512]{2,1,0:T(8,128)(2,1)}), bf16[32,16,512]{2,1,0:T(8,128)(2,1)S(1)}, u32[]{:S(2)}, u32[]{:S(2)}) async-start(bf16[32,16,512]{2,1,0:T(8,128)(2,1)} %bitcast.102), calls=%async_computation.1 | async-start | bytes 1048576 | tf_op jit(solution)/shard_map/all_to_all | solution.py:47
  113.7 11.4 %all-to-all-done.1 = bf16[32,16,512]{2,1,0:T(8,128)(2,1)S(1)} async-done(((bf16[32,16,512]{2,1,0:T(8,128)(2,1)}), bf16[32,16,512]{2,1,0:T(8,128)(2,1)S(1)}, u32[]{:S(2)}, u32[]{:S(2)}) %all-to-all-start.1) | async-done | bytes 524320 | tf_op jit(solution)/shard_map/all_to_all | solution.py:47
  125.1 0.1 convert_reduce_fusion.1
  125.2 0.0 copy-done.6
  125.2 1.5 fusion.11
  126.7 0.1 broadcast_in_dim.17
  126.7 15.5 %all_to_all.39 = bf16[32,16,512]{2,1,0:T(8,128)(2,1)S(1)} all-to-all(bf16[32,16,512]{2,1,0:T(8,128)(2,1)S(1)} %broadcast_in_dim.17), channel_id=1, replica_groups=mesh['rel'=8,'vrow'=32,'vcol'=4] {'rel','vcol'}, dimensions={0} | all-to-all | bytes 1048576 | tf_op jit(solution)/shard_map/all_to_all | solution.py:53
  142.3 0.0 copy-done.5
  142.3 1.1 fusion.5
  143.3 4.6 %all-to-all-start.3 = ((bf16[32,8,512]{2,1,0:T(8,128)(2,1)}), bf16[32,8,512]{2,1,0:T(8,128)(2,1)}, u32[]{:S(2)}, u32[]{:S(2)}) async-start(bf16[32,8,512]{2,1,0:T(8,128)(2,1)} %fusion.5), calls=%async_computation.3 | async-start | bytes 524288 | tf_op jit(solution)/shard_map/all_to_all | solution.py:42
  147.9 2.9 %convolution_convert_fusion.1 = bf16[512,2,512]{2,0,1:T(8,128)(2,1)} fusion(bf16[512,512,1]{1,0,2:T(8,128)(2,1)S(1)} %bitcast.101, bf16[2,512,512]{2,1,0:T(8,128)(2,1)} %param.15), kind=kOutput, calls=%fused_computation.5 | convolution fusion | flops 537395200 | bytes 2621440 | tf_op jit(solution)/shard_map/nf,sfh->nsh/dot_general | solution.py:11
  150.9 3.7 %gather_fusion.2 = bf16[24,128,512]{2,1,0:T(8,128)(2,1)} fusion(bf16[2,4,128,512]{3,2,1,0:T(8,128)(2,1)} %bitcast.98, s32[24]{0:T(128)S(1)} %reshape.48), kind=kCustom, calls=%fused_computation.2 | custom fusion | bytes 6291648 | tf_op jit(solution)/shard_map/vmap()/gather | solution.py:21
  154.5 35.2 %all-to-all-done.3 = bf16[32,8,512]{2,1,0:T(8,128)(2,1)} async-done(((bf16[32,8,512]{2,1,0:T(8,128)(2,1)}), bf16[32,8,512]{2,1,0:T(8,128)(2,1)}, u32[]{:S(2)}, u32[]{:S(2)}) %all-to-all-start.3) | async-done | bytes 262176 | tf_op jit(solution)/shard_map/all_to_all | solution.py:42
  189.8 1.7 convolution_convert_fusion.2
  191.5 2.5 %gather_fusion.3 = bf16[24,128,512]{2,1,0:T(8,128)(2,1)} fusion(bf16[2,2,128,512]{3,2,1,0:T(8,128)(2,1)S(1)} %bitcast.92, s32[24]{0:T(128)S(1)} %reshape.54), kind=kCustom, calls=%fused_computation.3 | custom fusion | bytes 6291648 | tf_op jit(solution)/shard_map/vmap()/gather | solution.py:21
  194.0 2.7 %convolution_bitcast_fusion = f32[4,128,512]{2,1,0:T(8,128)S(1)} fusion(bf16[2,4,3,128,512]{4,3,2,1,0:T(8,128)(2,1)} %bitcast.94, bf16[2,4,3,128,128]{4,3,2,1,0:T(8,128)(2,1)S(1)} %copy-done.3, bf16[2,4,3]{2,1,0:T(4,128)(2,1)S(1)} %copy.24, bf16[2,4,3]{2,1,0:T(4,128)(2,1)S(1)} %fusion.35), kind=kOutput, calls=%fused_computation.6 | convolution fusion | flops 403439616 | bytes 4980832 | tf_op jit(solution)/shard_map/sktab,sktbh->kah/dot_general | solution.py:28
  196.7 0.1 copy-done.1
  196.8 0.7 fusion.2
  197.5 16.5 %all_to_all.40 = bf16[32,16,512]{2,1,0:T(8,128)(2,1)S(1)} all-to-all(bf16[32,16,512]{2,1,0:T(8,128)(2,1)S(1)} %bitcast.103), channel_id=1, replica_groups=mesh['rel'=8,'vrow'=32,'vcol'=4] {'rel','vcol'}, dimensions={0} | all-to-all | bytes 1048576 | tf_op jit(solution)/shard_map/all_to_all | solution.py:47
  214.0 0.1 convert_reduce_fusion
  214.1 0.0 copy-done.4
  214.1 0.0 copy-done.7
  214.1 0.8 fusion.12
  (6 shorter events, 0.0 us)
Async XLA Ops:
  0.0 34.1 %copy-start = (bf16[2,1024,512]{2,1,0:T(8,128)(2,1)S(1)}, bf16[2,1024,512]{2,1,0:T(8,128)(2,1)}, u32[]{:S(2)}) copy-start(bf16[2,1024,512]{2,1,0:T(8,128)(2,1)} %param.12) | copy-start | bytes 6291460
  2.7 93.7 %all-to-all-start = ((bf16[32,8,1024]{2,1,0:T(8,128)(2,1)}), bf16[32,8,1024]{2,1,0:T(8,128)(2,1)}, u32[]{:S(2)}, u32[]{:S(2)}) async-start(bf16[32,8,1024]{2,1,0:T(8,128)(2,1)} %fusion.4), calls=%async_computation | async-start | bytes 1048576 | tf_op jit(solution)/shard_map/all_to_all | solution.py:42
  36.6 2.5 %copy-start.8 = (s32[2,4,1]{1,2,0:T(1,128)S(1)}, s32[2,4,1]{1,2,0:T(1,128)}, u32[]{:S(2)}) copy-start(s32[2,4,1]{1,2,0:T(1,128)} %param.20) | copy-start | bytes 100
  98.1 2.5 %copy-start.3 = (bf16[2,4,3,128,128]{4,3,2,1,0:T(8,128)(2,1)S(1)}, bf16[2,4,3,128,128]{4,3,2,1,0:T(8,128)(2,1)}, u32[]{:S(2)}) copy-start(bf16[2,4,3,128,128]{4,3,2,1,0:T(8,128)(2,1)} %param.18) | copy-start | bytes 2359300
  100.7 2.8 %copy-start.2 = (bf16[24,128,512]{2,1,0:T(8,128)(2,1)S(1)}, bf16[24,128,512]{2,1,0:T(8,128)(2,1)}, u32[]{:S(2)}) copy-start(bf16[24,128,512]{2,1,0:T(8,128)(2,1)} %gather_fusion) | copy-start | bytes 9437188
  103.5 21.7 %copy-start.6 = (f32[512]{0:T(512)S(1)}, f32[512]{0:T(512)}, u32[]{:S(2)}) copy-start(f32[512]{0:T(512)} %param.14) | copy-start | bytes 6148
  105.0 37.3 %copy-start.5 = (s32[1,1,1,256]{3,2,1,0:T(1,128)S(1)}, s32[1,1,1,256]{3,2,1,0:T(1,128)}, u32[]{:S(2)}) copy-start(s32[1,1,1,256]{3,2,1,0:T(1,128)} %param.21) | copy-start | bytes 3076
  105.0 20.1 %all-to-all-start.1 = ((bf16[32,16,512]{2,1,0:T(8,128)(2,1)}), bf16[32,16,512]{2,1,0:T(8,128)(2,1)S(1)}, u32[]{:S(2)}, u32[]{:S(2)}) async-start(bf16[32,16,512]{2,1,0:T(8,128)(2,1)} %bitcast.102), calls=%async_computation.1 | async-start | bytes 1048576 | tf_op jit(solution)/shard_map/all_to_all | solution.py:47
  143.3 46.4 %all-to-all-start.3 = ((bf16[32,8,512]{2,1,0:T(8,128)(2,1)}), bf16[32,8,512]{2,1,0:T(8,128)(2,1)}, u32[]{:S(2)}, u32[]{:S(2)}) async-start(bf16[32,8,512]{2,1,0:T(8,128)(2,1)} %fusion.5), calls=%async_computation.3 | async-start | bytes 524288 | tf_op jit(solution)/shard_map/all_to_all | solution.py:42
  194.0 2.8 %copy-start.1 = (bf16[24,128,512]{2,1,0:T(8,128)(2,1)S(1)}, bf16[24,128,512]{2,1,0:T(8,128)(2,1)}, u32[]{:S(2)}) copy-start(bf16[24,128,512]{2,1,0:T(8,128)(2,1)} %gather_fusion.2) | copy-start | bytes 9437188
  196.8 17.2 %copy-start.4 = (bf16[512,512]{1,0:T(8,128)(2,1)S(1)}, bf16[512,512]{1,0:T(8,128)(2,1)}, u32[]{:S(2)}) copy-start(bf16[512,512]{1,0:T(8,128)(2,1)} %param.16) | copy-start | bytes 1572868
  196.8 17.2 %copy-start.7 = (f32[512]{0:T(512)S(1)}, f32[512]{0:T(512)}, u32[]{:S(2)}) copy-start(f32[512]{0:T(512)} %param.17) | copy-start | bytes 6148

commit v5 on v4

--- a/solution.py
+++ b/solution.py
@@ -29,11 +29,19 @@
     return summed.reshape(-1, summed.shape[-1])
 
 
-def layer_part(own_rows, far_rows, weight, local_tiles, remote_tiles, local_pick, remote_pick):
+def far_aggregate(far_proj, remote_dense):
+    blocks = remote_dense.shape[3]
+    rows = far_proj.reshape(blocks, far_proj.shape[0] // blocks, far_proj.shape[1], far_proj.shape[2])
+    summed = jnp.einsum("rkasb,sbrh->kah", remote_dense, rows.astype(jnp.float32),
+                        precision=lax.Precision.HIGHEST, preferred_element_type=jnp.float32)
+    return summed.reshape(-1, summed.shape[-1])
+
+
+def layer_part(own_rows, far_rows, weight, local_tiles, remote_dense, local_pick):
     own_proj = project(own_rows, weight)
     own_sum = aggregate(own_proj, local_tiles, local_pick)
     far_proj = project(far_rows, weight)
-    return own_sum + aggregate(far_proj, remote_tiles, remote_pick)
+    return own_sum + far_aggregate(far_proj, remote_dense)
 
 
 def fetch_rows(values, send_index):
@@ -79,19 +87,23 @@
     local_tiles = masked * is_local.astype(tiles.dtype)[:, :, :, None, None]
     remote_tiles = masked * (~is_local).astype(tiles.dtype)[:, :, :, None, None]
     local_pick = jnp.where(is_local, tile_source, 0)
-    remote_pick = jnp.where(is_local, 0, tile_source - local_rows_blocks)
+    remote_pick = jnp.where(is_local, -1, tile_source - local_rows_blocks)
+    remote_blocks = send_index.shape[0] // tiles.shape[-1]
+    remote_choice = (remote_pick[..., None] == jnp.arange(remote_blocks, dtype=remote_pick.dtype)).astype(jnp.float32)
+    remote_dense = jnp.einsum("rktab,rkts->rkasb", remote_tiles.astype(jnp.float32), remote_choice,
+                              precision=lax.Precision.HIGHEST)
     parts = lax.axis_size(GROUP)
     share_rows = local_rows // parts
     row_start = lax.axis_index(GROUP) * share_rows
     received = fetch_rows(features, send_index)
-    first_part = layer_part(features, received, first_weight, local_tiles, remote_tiles, local_pick, remote_pick)
+    first_part = layer_part(features, received, first_weight, local_tiles, remote_dense, local_pick)
     first_share = scatter_sum(first_part.astype(jnp.bfloat16), parts)
     own_features = lax.dynamic_slice_in_dim(features, row_start, share_rows, 0)
     first_term = jnp.dot(own_features, first_root, preferred_element_type=jnp.float32)
     hidden_share = jax.nn.relu(first_share + first_term + first_bias).astype(jnp.bfloat16)
     hidden = gather_all(hidden_share, parts)
     received_hidden = fetch_rows(hidden, send_index)
-    second_part = layer_part(hidden, received_hidden, second_weight, local_tiles, remote_tiles, local_pick, remote_pick)
+    second_part = layer_part(hidden, received_hidden, second_weight, local_tiles, remote_dense, local_pick)
     second_share = scatter_sum(second_part.astype(jnp.bfloat16), parts)
     second_term = jnp.dot(hidden_share, second_root, preferred_element_type=jnp.float32)
     result = jax.nn.relu(second_share + second_term + second_bias).astype(jnp.bfloat16)

time: 216 us -> 208 us (0.963)
  waiting for transfers between devices: 104 us -> 94.4 us
  local copies, waits for them, and re-layouts: 12.1 us -> 7.54 us
  matrix products: 22.5 us -> 26.4 us
  other arithmetic: 1.64 us -> 4.8 us
    all_to_all x2, waiting for transfers between devices: 92.5 us -> 83 us  [fetch_rows(): lax.all_to_all(outgoing, 'vrow', split_axis=0, concat_axis=0, tiled=True)]
    gather x8 -> x4, local copies, waits for them, and re-layouts: 11.5 us -> 6.31 us  [pick(): return source_blocks[indices]]
    dot_general x0 -> x3, matrix products: none -> 4.78 us  [the longest x2 3.99 us: far_aggregate(): jnp.einsum('rkasb,sbrh->kah', remote_dense, rows.astype(jnp.float32), pre...]
    dot_general x4 -> x2, matrix products: 7.53 us -> 6.54 us  [aggregate(): jnp.einsum('sktab,sktbh->kah', weighted, picked, preferred_element_type=j...]
  transfers between devices with their start and end apart: 3 -> 3, of which waited for: 3 -> 3; matrix products, arithmetic and copies ran while one was open for 6% -> 11% of each run, Pallas kernels for 0% -> 0%
where the time goes in v5:
time: 208 us; the launch traced here: 207 us
  waiting for transfers between devices  94.4 us (45%)
  starting transfers between devices  41.9 us (20%)
  blocking collectives  32 us (15%)
  matrix products  26.4 us (13%)
  local copies, waits for them, and re-layouts  7.54 us (4%)
  other arithmetic  4.8 us (2%)
    all_to_all x2, waiting for transfers between devices, fetch_rows(): lax.all_to_all(outgoing, 'vrow', split_axis=0, concat_axis=0, tiled=True)  83 us
    all_to_all x2, starting transfers between devices, fetch_rows(): lax.all_to_all(outgoing, 'vrow', split_axis=0, concat_axis=0, tiled=True)  33.3 us
    all_to_all x1, blocking collectives, scatter_sum(): received = lax.all_to_all(chunks, GROUP, 0, 0, tiled=False)  16.5 us
    all_to_all x1, blocking collectives, gather_all(): received = lax.all_to_all(copies, GROUP, 0, 0, tiled=False)  15.5 us
    all_to_all x1, waiting for transfers between devices, scatter_sum(): received = lax.all_to_all(chunks, GROUP, 0, 0, tiled=False)  11.5 us
    dot_general x4, matrix products, project(): jnp.einsum('nf,sfh->nsh', row_values, weight, preferred_element_type=jnp....  9.1 us
    all_to_all x1, starting transfers between devices, scatter_sum(): received = lax.all_to_all(chunks, GROUP, 0, 0, tiled=False)  8.61 us
    dot_general x2, matrix products, aggregate(): jnp.einsum('sktab,sktbh->kah', weighted, picked, preferred_element_type=j...  6.54 us
  transfers between devices with their start and end apart: 3, of which 3 were waited for; matrix products, arithmetic and copies ran while one was open for 11% of the time, Pallas kernels for 0%

profile of v5, /device:TPU:1, one launch (start us, length us, event | category | flops | bytes accessed | tf_op | source)
XLA Modules:
  0.0 207.2 jit_solution(2232405005606040871)
XLA Ops:
  0.0 0.0 copy-start
  0.0 2.7 %fusion.4 = bf16[32,8,1024]{2,1,0:T(8,128)(2,1)} fusion(bf16[512,1024]{1,0:T(8,128)(2,1)} %param.11, s32[256]{0:T(256)} %bitcast.104), kind=kOutput, calls=%fused_computation.13 | convolution fusion | flops 268828672 | bytes 1573888 | tf_op jit(solution)/shard_map/dot_general | solution.py:49
  2.7 29.4 %all-to-all-start = ((bf16[32,8,1024]{2,1,0:T(8,128)(2,1)}), bf16[32,8,1024]{2,1,0:T(8,128)(2,1)}, u32[]{:S(2)}, u32[]{:S(2)}) async-start(bf16[32,8,1024]{2,1,0:T(8,128)(2,1)} %fusion.4), calls=%async_computation | async-start | bytes 1048576 | tf_op jit(solution)/shard_map/all_to_all | solution.py:50
  32.1 0.7 add_select_fusion
  32.8 0.1 copy.25
  32.9 0.7 fusion.41
  33.6 0.1 copy.22
  33.7 0.1 reshape.55
  33.7 0.7 not_convert_fusion
  34.4 0.1 copy.26
  34.6 0.1 copy.21
  34.7 0.0 copy-done
  34.7 2.5 %convolution_convert_fusion = bf16[512,2,512]{2,0,1:T(8,128)(2,1)S(1)} fusion(bf16[2,1024,512]{2,1,0:T(8,128)(2,1)S(1)} %copy-done, bf16[512,1024]{1,0:T(8,128)(2,1)} %param.11), kind=kOutput, calls=%fused_computation.2 | convolution fusion | flops 1074266112 | bytes 4194304 | tf_op jit(solution)/shard_map/nf,sfh->nsh/dot_general | solution.py:11
  37.1 0.0 copy-start.8
  37.2 2.5 %gather_fusion = bf16[24,128,512]{2,1,0:T(8,128)(2,1)} fusion(bf16[2,4,128,512]{3,2,1,0:T(8,128)(2,1)S(1)} %bitcast.95, s32[24]{0:T(128)S(1)} %reshape.55), kind=kCustom, calls=%fused_computation | custom fusion | bytes 6291648 | tf_op jit(solution)/shard_map/vmap()/gather | solution.py:21
  39.6 0.0 copy-done.8
  39.6 0.1 fusion.37
  39.7 1.4 multiply_multiply_fusion
  41.1 0.8 fusion.14
  41.9 0.0 copy-done.1
  41.9 2.8 %fusion.20 = f32[4,128,512,1,1]{2,1,4,0,3:T(8,128)} fusion(bf16[2,4,3,128,512]{4,3,2,1,0:T(8,128)(2,1)S(1)} %bitcast.90, bf16[2,4,3,128,128]{4,3,2,1,0:T(8,128)(2,1)} %param.18, bf16[2,4,3]{2,1,0:T(4,128)(2,1)S(1)} %copy.21, bf16[2,4,3]{2,1,0:T(4,128)(2,1)S(1)} %fusion.37), kind=kOutput, calls=%fused_computation.34 | convolution fusion | flops 403439616 | bytes 4980832 | tf_op jit(solution)/shard_map/sktab,sktbh->kah/dot_general | solution.py:28
  44.7 51.7 %all-to-all-done = bf16[32,8,1024]{2,1,0:T(8,128)(2,1)} async-done(((bf16[32,8,1024]{2,1,0:T(8,128)(2,1)}), bf16[32,8,1024]{2,1,0:T(8,128)(2,1)}, u32[]{:S(2)}, u32[]{:S(2)}) %all-to-all-start) | async-done | bytes 524320 | tf_op jit(solution)/shard_map/all_to_all | solution.py:50
  96.4 1.8 convolution_convert_fusion.4
  98.2 0.0 copy-start.6
  98.2 0.0 copy-done.2
  98.2 0.0 copy-start.5
  98.3 1.8 fusion.3
  100.0 8.6 %all-to-all-start.1 = ((bf16[32,16,512]{2,1,0:T(8,128)(2,1)}), bf16[32,16,512]{2,1,0:T(8,128)(2,1)}, u32[]{:S(2)}, u32[]{:S(2)}) async-start(bf16[32,16,512]{2,1,0:T(8,128)(2,1)} %bitcast.101), calls=%async_computation.1 | async-start | bytes 1048576 | tf_op jit(solution)/shard_map/all_to_all | solution.py:55
  108.7 11.5 %all-to-all-done.1 = bf16[32,16,512]{2,1,0:T(8,128)(2,1)} async-done(((bf16[32,16,512]{2,1,0:T(8,128)(2,1)}), bf16[32,16,512]{2,1,0:T(8,128)(2,1)}, u32[]{:S(2)}, u32[]{:S(2)}) %all-to-all-start.1) | async-done | bytes 524320 | tf_op jit(solution)/shard_map/all_to_all | solution.py:55
  120.1 1.1 convert_reduce_fusion.1
  121.3 0.0 copy-done.6
  121.3 1.5 fusion.11
  122.8 0.1 broadcast_in_dim.17
  122.8 15.5 %all_to_all.39 = bf16[32,16,512]{2,1,0:T(8,128)(2,1)S(1)} all-to-all(bf16[32,16,512]{2,1,0:T(8,128)(2,1)S(1)} %broadcast_in_dim.17), channel_id=1, replica_groups=mesh['rel'=8,'vrow'=32,'vcol'=4] {'rel','vcol'}, dimensions={0} | all-to-all | bytes 1048576 | tf_op jit(solution)/shard_map/all_to_all | solution.py:61
  138.4 0.8 copy-done.3
  139.1 0.0 copy-done.5
  139.1 1.1 fusion.5
  140.2 3.9 %all-to-all-start.3 = ((bf16[32,8,512]{2,1,0:T(8,128)(2,1)}), bf16[32,8,512]{2,1,0:T(8,128)(2,1)S(1)}, u32[]{:S(2)}, u32[]{:S(2)}) async-start(bf16[32,8,512]{2,1,0:T(8,128)(2,1)} %fusion.5), calls=%async_computation.3 | async-start | bytes 524288 | tf_op jit(solution)/shard_map/all_to_all | solution.py:50
  144.1 3.1 %convolution_convert_fusion.1 = bf16[512,2,512]{2,0,1:T(8,128)(2,1)} fusion(bf16[512,512,1]{1,0,2:T(8,128)(2,1)} %bitcast.99, bf16[2,512,512]{2,1,0:T(8,128)(2,1)} %param.15), kind=kOutput, calls=%fused_computation.3 | convolution fusion | flops 537395200 | bytes 2621440 | tf_op jit(solution)/shard_map/nf,sfh->nsh/dot_general | solution.py:11
  147.2 3.7 %gather_fusion.1 = bf16[24,128,512]{2,1,0:T(8,128)(2,1)} fusion(bf16[2,4,128,512]{3,2,1,0:T(8,128)(2,1)} %bitcast.94, s32[24]{0:T(128)S(1)} %reshape.55), kind=kCustom, calls=%fused_computation.1 | custom fusion | bytes 6291648 | tf_op jit(solution)/shard_map/vmap()/gather | solution.py:21
  150.8 3.8 %fusion.18 = f32[4,128,512,1,1]{2,1,4,0,3:T(8,128)} fusion(bf16[2,4,3,128,512]{4,3,2,1,0:T(8,128)(2,1)} %bitcast.91, bf16[2,4,3,128,128]{4,3,2,1,0:T(8,128)(2,1)} %param.18, bf16[2,4,3]{2,1,0:T(4,128)(2,1)S(1)} %copy.21, bf16[2,4,3]{2,1,0:T(4,128)(2,1)S(1)} %fusion.37), kind=kOutput, calls=%fused_computation.32 | convolution fusion | flops 403439616 | bytes 4980832 | tf_op jit(solution)/shard_map/sktab,sktbh->kah/dot_general | solution.py:28
  154.6 31.3 %all-to-all-done.3 = bf16[32,8,512]{2,1,0:T(8,128)(2,1)S(1)} async-done(((bf16[32,8,512]{2,1,0:T(8,128)(2,1)}), bf16[32,8,512]{2,1,0:T(8,128)(2,1)S(1)}, u32[]{:S(2)}, u32[]{:S(2)}) %all-to-all-start.3) | async-done | bytes 262176 | tf_op jit(solution)/shard_map/all_to_all | solution.py:50
  185.9 1.7 convolution_convert_fusion.2
  187.6 2.2 %fusion.2 = bf16[512,512]{1,0:T(8,128)(2,1)S(1)} fusion(f32[512,512]{1,0:T(8,128)} %bitcast.96, bf16[2,128,2,512]{3,1,0,2:T(8,128)(2,1)S(1)} %bitcast.100, f32[512,128,2,2]{1,3,0,2:T(2,128)S(1)} %bitcast.93), kind=kOutput, calls=%fused_computation.8 | convolution fusion | flops 1611137024 | bytes 3145728 | tf_op jit(solution)/shard_map/rkasb,sbrh->kah/dot_general | solution.py:35
  189.9 16.5 %all_to_all.40 = bf16[32,16,512]{2,1,0:T(8,128)(2,1)S(1)} all-to-all(bf16[32,16,512]{2,1,0:T(8,128)(2,1)S(1)} %bitcast.102), channel_id=1, replica_groups=mesh['rel'=8,'vrow'=32,'vcol'=4] {'rel','vcol'}, dimensions={0} | all-to-all | bytes 1048576 | tf_op jit(solution)/shard_map/all_to_all | solution.py:55
  206.3 0.1 convert_reduce_fusion
  206.4 0.0 copy-done.7
  206.4 0.8 fusion.12
  (6 shorter events, 0.0 us)
Async XLA Ops:
  0.0 34.7 %copy-start = (bf16[2,1024,512]{2,1,0:T(8,128)(2,1)S(1)}, bf16[2,1024,512]{2,1,0:T(8,128)(2,1)}, u32[]{:S(2)}) copy-start(bf16[2,1024,512]{2,1,0:T(8,128)(2,1)} %param.12) | copy-start | bytes 6291460
  2.7 93.7 %all-to-all-start = ((bf16[32,8,1024]{2,1,0:T(8,128)(2,1)}), bf16[32,8,1024]{2,1,0:T(8,128)(2,1)}, u32[]{:S(2)}, u32[]{:S(2)}) async-start(bf16[32,8,1024]{2,1,0:T(8,128)(2,1)} %fusion.4), calls=%async_computation | async-start | bytes 1048576 | tf_op jit(solution)/shard_map/all_to_all | solution.py:50
  37.1 2.5 %copy-start.8 = (s32[2,4,1]{1,2,0:T(1,128)S(1)}, s32[2,4,1]{1,2,0:T(1,128)}, u32[]{:S(2)}) copy-start(s32[2,4,1]{1,2,0:T(1,128)} %param.20) | copy-start | bytes 100
  39.6 2.3 %copy-start.1 = (bf16[24,128,512]{2,1,0:T(8,128)(2,1)S(1)}, bf16[24,128,512]{2,1,0:T(8,128)(2,1)}, u32[]{:S(2)}) copy-start(bf16[24,128,512]{2,1,0:T(8,128)(2,1)} %gather_fusion) | copy-start | bytes 9437188
  96.4 1.9 copy-start.2
  98.2 23.0 %copy-start.6 = (f32[512]{0:T(512)S(1)}, f32[512]{0:T(512)}, u32[]{:S(2)}) copy-start(f32[512]{0:T(512)} %param.14) | copy-start | bytes 6148
  98.2 40.9 %copy-start.5 = (s32[1,1,1,256]{3,2,1,0:T(1,128)S(1)}, s32[1,1,1,256]{3,2,1,0:T(1,128)}, u32[]{:S(2)}) copy-start(s32[1,1,1,256]{3,2,1,0:T(1,128)} %param.21) | copy-start | bytes 3076
  100.0 20.1 %all-to-all-start.1 = ((bf16[32,16,512]{2,1,0:T(8,128)(2,1)}), bf16[32,16,512]{2,1,0:T(8,128)(2,1)}, u32[]{:S(2)}, u32[]{:S(2)}) async-start(bf16[32,16,512]{2,1,0:T(8,128)(2,1)} %bitcast.101), calls=%async_computation.1 | async-start | bytes 1048576 | tf_op jit(solution)/shard_map/all_to_all | solution.py:55
  138.4 0.8 copy-start.3
  140.2 45.7 %all-to-all-start.3 = ((bf16[32,8,512]{2,1,0:T(8,128)(2,1)}), bf16[32,8,512]{2,1,0:T(8,128)(2,1)S(1)}, u32[]{:S(2)}, u32[]{:S(2)}) async-start(bf16[32,8,512]{2,1,0:T(8,128)(2,1)} %fusion.5), calls=%async_computation.3 | async-start | bytes 524288 | tf_op jit(solution)/shard_map/all_to_all | solution.py:50
  154.6 51.8 %copy-start.7 = (f32[512]{0:T(512)S(1)}, f32[512]{0:T(512)}, u32[]{:S(2)}) copy-start(f32[512]{0:T(512)} %param.17) | copy-start | bytes 6148
  185.9 20.5 %copy-start.4 = (bf16[512,512]{1,0:T(8,128)(2,1)S(1)}, bf16[512,512]{1,0:T(8,128)(2,1)}, u32[]{:S(2)}) copy-start(bf16[512,512]{1,0:T(8,128)(2,1)} %param.16) | copy-start | bytes 1572868

commit v6 on v5

--- a/solution.py
+++ b/solution.py
@@ -46,7 +46,7 @@
 
 def fetch_rows(values, send_index):
     chooser = (send_index[:, None] == jnp.arange(values.shape[0], dtype=send_index.dtype)[None, :])
-    outgoing = jnp.dot(chooser.astype(values.dtype), values, preferred_element_type=jnp.float32).astype(values.dtype)
+    outgoing = jnp.dot(chooser.astype(values.dtype), values, preferred_element_type=values.dtype)
     return lax.all_to_all(outgoing, "vrow", split_axis=0, concat_axis=0, tiled=True)
 
 

time: 208 us -> 210 us (level)
  blocking collectives: 32 us -> 16.4 us
  waiting for transfers between devices: 94.4 us -> 105 us
  starting transfers between devices: 41.9 us -> 46.5 us
    all_to_all x1 -> x0, blocking collectives: 15.5 us -> none  [gather_all(): received = lax.all_to_all(copies, GROUP, 0, 0, tiled=False)]
    all_to_all x0 -> x1, waiting for transfers between devices: none -> 10.3 us  [gather_all(): received = lax.all_to_all(copies, GROUP, 0, 0, tiled=False)]
    all_to_all x0 -> x1, starting transfers between devices: none -> 4.64 us  [gather_all(): received = lax.all_to_all(copies, GROUP, 0, 0, tiled=False)]
  transfers between devices with their start and end apart: 3 -> 4, of which waited for: 3 -> 4; matrix products, arithmetic and copies ran while one was open for 11% -> 12% of each run, Pallas kernels for 0% -> 0%
where the time goes in v6:
time: 210 us; the launch traced here: 209 us
  waiting for transfers between devices  105 us (50%)
  starting transfers between devices  46.5 us (22%)
  matrix products  27.5 us (13%)
  blocking collectives  16.4 us (8%)
  local copies, waits for them, and re-layouts  8.17 us (4%)
  other arithmetic  5.47 us (3%)
    all_to_all x2, waiting for transfers between devices, fetch_rows(): lax.all_to_all(outgoing, 'vrow', split_axis=0, concat_axis=0, tiled=True)  83 us
    all_to_all x2, starting transfers between devices, fetch_rows(): lax.all_to_all(outgoing, 'vrow', split_axis=0, concat_axis=0, tiled=True)  33.3 us
    all_to_all x1, blocking collectives, scatter_sum(): received = lax.all_to_all(chunks, GROUP, 0, 0, tiled=False)  16.4 us
    all_to_all x1, waiting for transfers between devices, scatter_sum(): received = lax.all_to_all(chunks, GROUP, 0, 0, tiled=False)  11.5 us
    all_to_all x1, waiting for transfers between devices, gather_all(): received = lax.all_to_all(copies, GROUP, 0, 0, tiled=False)  10.3 us
    dot_general x4, matrix products, project(): jnp.einsum('nf,sfh->nsh', row_values, weight, preferred_element_type=jnp....  9.1 us
    all_to_all x1, starting transfers between devices, scatter_sum(): received = lax.all_to_all(chunks, GROUP, 0, 0, tiled=False)  8.61 us
    dot_general x2, matrix products, aggregate(): jnp.einsum('sktab,sktbh->kah', weighted, picked, preferred_element_type=j...  6.54 us
  transfers between devices with their start and end apart: 4, of which 4 were waited for; matrix products, arithmetic and copies ran while one was open for 12% of the time, Pallas kernels for 0%

profile of v6, /device:TPU:1, one launch (start us, length us, event | category | flops | bytes accessed | tf_op | source)
XLA Modules:
  0.0 209.0 jit_solution(12273025467735746093)
XLA Ops:
  0.0 0.0 copy-start
  0.0 2.7 %convolution_bitcast_fusion.2 = bf16[32,8,1024]{2,1,0:T(8,128)(2,1)} fusion(bf16[512,1024]{1,0:T(8,128)(2,1)} %param.11, s32[256]{0:T(256)} %bitcast.103), kind=kOutput, calls=%fused_computation.12 | convolution fusion | flops 268566528 | bytes 1573888 | tf_op jit(solution)/shard_map/dot_general | solution.py:49
  2.7 29.4 %all-to-all-start = ((bf16[32,8,1024]{2,1,0:T(8,128)(2,1)}), bf16[32,8,1024]{2,1,0:T(8,128)(2,1)}, u32[]{:S(2)}, u32[]{:S(2)}) async-start(bf16[32,8,1024]{2,1,0:T(8,128)(2,1)} %convolution_bitcast_fusion.2), calls=%async_computation | async-start | bytes 1048576 | tf_op jit(solution)/shard_map/all_to_all | solution.py:50
  32.1 0.7 not_convert_fusion
  32.8 0.1 copy.21
  32.9 0.7 fusion.42
  33.6 0.1 copy.22
  33.7 0.1 reshape.78
  33.8 0.1 copy.26
  33.9 0.7 add_select_fusion
  34.6 0.1 copy.25
  34.7 0.0 copy-done
  34.7 2.5 %convolution_convert_fusion = bf16[512,2,512]{2,0,1:T(8,128)(2,1)S(1)} fusion(bf16[2,1024,512]{2,1,0:T(8,128)(2,1)S(1)} %copy-done, bf16[512,1024]{1,0:T(8,128)(2,1)} %param.11), kind=kOutput, calls=%fused_computation.2 | convolution fusion | flops 1074266112 | bytes 4194304 | tf_op jit(solution)/shard_map/nf,sfh->nsh/dot_general | solution.py:11
  37.1 0.0 copy-start.7
  37.2 2.5 %gather_fusion = bf16[24,128,512]{2,1,0:T(8,128)(2,1)} fusion(bf16[2,4,128,512]{3,2,1,0:T(8,128)(2,1)S(1)} %bitcast.96, s32[24]{0:T(128)S(1)} %reshape.78), kind=kCustom, calls=%fused_computation | custom fusion | bytes 6291648 | tf_op jit(solution)/shard_map/vmap()/gather | solution.py:21
  39.6 0.0 copy-done.7
  39.6 0.1 fusion.38
  39.7 1.4 multiply_multiply_fusion
  41.1 0.8 fusion.12
  41.9 0.0 copy-done.1
  41.9 2.8 %fusion.18 = f32[4,128,512,1,1]{2,1,4,0,3:T(8,128)} fusion(bf16[2,4,3,128,512]{4,3,2,1,0:T(8,128)(2,1)S(1)} %bitcast.91, bf16[2,4,3,128,128]{4,3,2,1,0:T(8,128)(2,1)} %param.18, bf16[2,4,3]{2,1,0:T(4,128)(2,1)S(1)} %copy.21, bf16[2,4,3]{2,1,0:T(4,128)(2,1)S(1)} %fusion.38), kind=kOutput, calls=%fused_computation.31 | convolution fusion | flops 403439616 | bytes 4980832 | tf_op jit(solution)/shard_map/sktab,sktbh->kah/dot_general | solution.py:28
  44.7 51.7 %all-to-all-done = bf16[32,8,1024]{2,1,0:T(8,128)(2,1)} async-done(((bf16[32,8,1024]{2,1,0:T(8,128)(2,1)}), bf16[32,8,1024]{2,1,0:T(8,128)(2,1)}, u32[]{:S(2)}, u32[]{:S(2)}) %all-to-all-start) | async-done | bytes 524320 | tf_op jit(solution)/shard_map/all_to_all | solution.py:50
  96.4 1.8 convolution_convert_fusion.3
  98.2 0.0 copy-start.5
  98.2 0.0 copy-done.2
  98.2 0.0 copy-start.4
  98.3 1.8 fusion.3
  100.1 8.6 %all-to-all-start.1 = ((bf16[32,16,512]{2,1,0:T(8,128)(2,1)}), bf16[32,16,512]{2,1,0:T(8,128)(2,1)}, u32[]{:S(2)}, u32[]{:S(2)}) async-start(bf16[32,16,512]{2,1,0:T(8,128)(2,1)} %bitcast.100), calls=%async_computation.1 | async-start | bytes 1048576 | tf_op jit(solution)/shard_map/all_to_all | solution.py:55
  108.7 11.5 %all-to-all-done.1 = bf16[32,16,512]{2,1,0:T(8,128)(2,1)} async-done(((bf16[32,16,512]{2,1,0:T(8,128)(2,1)}), bf16[32,16,512]{2,1,0:T(8,128)(2,1)}, u32[]{:S(2)}, u32[]{:S(2)}) %all-to-all-start.1) | async-done | bytes 524320 | tf_op jit(solution)/shard_map/all_to_all | solution.py:55
  120.1 1.1 convert_reduce_fusion.1
  121.3 1.5 fusion.9
  122.8 0.9 broadcast_in_dim.17
  123.7 4.6 %all-to-all-start.2 = ((bf16[32,16,512]{2,1,0:T(8,128)(2,1)}), bf16[32,16,512]{2,1,0:T(8,128)(2,1)}, u32[]{:S(2)}, u32[]{:S(2)}) async-start(bf16[32,16,512]{2,1,0:T(8,128)(2,1)} %broadcast_in_dim.17), calls=%async_computation.2 | async-start | bytes 1048576 | tf_op jit(solution)/shard_map/all_to_all | solution.py:61
  128.3 0.5 broadcast.90
  128.8 0.7 reduce.3
  129.5 0.1 eq.66
  129.6 10.3 %all-to-all-done.2 = bf16[32,16,512]{2,1,0:T(8,128)(2,1)} async-done(((bf16[32,16,512]{2,1,0:T(8,128)(2,1)}), bf16[32,16,512]{2,1,0:T(8,128)(2,1)}, u32[]{:S(2)}, u32[]{:S(2)}) %all-to-all-start.2) | async-done | bytes 524320 | tf_op jit(solution)/shard_map/all_to_all | solution.py:61
  139.9 2.1 %fusion.24 = bf16[32,8,512]{2,1,0:T(8,128)(2,1)} fusion(bf16[512,512,1]{1,0,2:T(8,128)(2,1)} %bitcast.22, s32[32,8]{1,0:T(8,128)S(1)} %eq.66), kind=kOutput, calls=%fused_computation.40 | convolution fusion | flops 134348800 | bytes 787456 | tf_op jit(solution)/shard_map/dot_general | solution.py:49
  142.0 3.9 %all-to-all-start.3 = ((bf16[32,8,512]{2,1,0:T(8,128)(2,1)}), bf16[32,8,512]{2,1,0:T(8,128)(2,1)S(1)}, u32[]{:S(2)}, u32[]{:S(2)}) async-start(bf16[32,8,512]{2,1,0:T(8,128)(2,1)} %fusion.24), calls=%async_computation.3 | async-start | bytes 524288 | tf_op jit(solution)/shard_map/all_to_all | solution.py:50
  145.8 3.1 %convolution_convert_fusion.1 = bf16[512,2,512]{2,0,1:T(8,128)(2,1)} fusion(bf16[512,512,1]{1,0,2:T(8,128)(2,1)} %bitcast.22, bf16[2,512,512]{2,1,0:T(8,128)(2,1)} %param.15), kind=kOutput, calls=%fused_computation.3 | convolution fusion | flops 537395200 | bytes 2621440 | tf_op jit(solution)/shard_map/nf,sfh->nsh/dot_general | solution.py:11
  148.9 3.7 %gather_fusion.1 = bf16[24,128,512]{2,1,0:T(8,128)(2,1)} fusion(bf16[2,4,128,512]{3,2,1,0:T(8,128)(2,1)} %bitcast.95, s32[24]{0:T(128)S(1)} %reshape.78), kind=kCustom, calls=%fused_computation.1 | custom fusion | bytes 6291648 | tf_op jit(solution)/shard_map/vmap()/gather | solution.py:21
  152.6 3.8 %fusion.16 = f32[4,128,512,1,1]{2,1,4,0,3:T(8,128)} fusion(bf16[2,4,3,128,512]{4,3,2,1,0:T(8,128)(2,1)} %bitcast.92, bf16[2,4,3,128,128]{4,3,2,1,0:T(8,128)(2,1)} %param.18, bf16[2,4,3]{2,1,0:T(4,128)(2,1)S(1)} %copy.21, bf16[2,4,3]{2,1,0:T(4,128)(2,1)S(1)} %fusion.38), kind=kOutput, calls=%fused_computation.29 | convolution fusion | flops 403439616 | bytes 4980832 | tf_op jit(solution)/shard_map/sktab,sktbh->kah/dot_general | solution.py:28
  156.4 31.3 %all-to-all-done.3 = bf16[32,8,512]{2,1,0:T(8,128)(2,1)S(1)} async-done(((bf16[32,8,512]{2,1,0:T(8,128)(2,1)}), bf16[32,8,512]{2,1,0:T(8,128)(2,1)S(1)}, u32[]{:S(2)}, u32[]{:S(2)}) %all-to-all-start.3) | async-done | bytes 262176 | tf_op jit(solution)/shard_map/all_to_all | solution.py:50
  187.7 1.7 convolution_convert_fusion.2
  189.4 2.2 %fusion.2 = bf16[512,512]{1,0:T(8,128)(2,1)S(1)} fusion(f32[512,512]{1,0:T(8,128)} %bitcast.97, bf16[2,128,2,512]{3,1,0,2:T(8,128)(2,1)S(1)} %bitcast.99, f32[512,128,2,2]{1,3,0,2:T(2,128)S(1)} %bitcast.94), kind=kOutput, calls=%fused_computation.8 | convolution fusion | flops 1611137024 | bytes 3145728 | tf_op jit(solution)/shard_map/rkasb,sbrh->kah/dot_general | solution.py:35
  191.6 16.4 %all_to_all.36 = bf16[32,16,512]{2,1,0:T(8,128)(2,1)S(1)} all-to-all(bf16[32,16,512]{2,1,0:T(8,128)(2,1)S(1)} %bitcast.101), channel_id=1, replica_groups=mesh['rel'=8,'vrow'=32,'vcol'=4] {'rel','vcol'}, dimensions={0} | all-to-all | bytes 1048576 | tf_op jit(solution)/shard_map/all_to_all | solution.py:55
  208.1 0.1 convert_reduce_fusion
  208.2 0.8 fusion.10
  (8 shorter events, 0.0 us)
Async XLA Ops:
  0.0 34.7 %copy-start = (bf16[2,1024,512]{2,1,0:T(8,128)(2,1)S(1)}, bf16[2,1024,512]{2,1,0:T(8,128)(2,1)}, u32[]{:S(2)}) copy-start(bf16[2,1024,512]{2,1,0:T(8,128)(2,1)} %param.12) | copy-start | bytes 6291460
  2.7 93.7 %all-to-all-start = ((bf16[32,8,1024]{2,1,0:T(8,128)(2,1)}), bf16[32,8,1024]{2,1,0:T(8,128)(2,1)}, u32[]{:S(2)}, u32[]{:S(2)}) async-start(bf16[32,8,1024]{2,1,0:T(8,128)(2,1)} %convolution_bitcast_fusion.2), calls=%async_computation | async-start | bytes 1048576 | tf_op jit(solution)/shard_map/all_to_all | solution.py:50
  37.1 2.5 %copy-start.7 = (s32[2,4,1]{1,2,0:T(1,128)S(1)}, s32[2,4,1]{1,2,0:T(1,128)}, u32[]{:S(2)}) copy-start(s32[2,4,1]{1,2,0:T(1,128)} %param.20) | copy-start | bytes 100
  39.6 2.3 %copy-start.1 = (bf16[24,128,512]{2,1,0:T(8,128)(2,1)S(1)}, bf16[24,128,512]{2,1,0:T(8,128)(2,1)}, u32[]{:S(2)}) copy-start(bf16[24,128,512]{2,1,0:T(8,128)(2,1)} %gather_fusion) | copy-start | bytes 9437188
  96.4 1.9 copy-start.2
  98.2 23.1 %copy-start.5 = (f32[512]{0:T(512)S(1)}, f32[512]{0:T(512)}, u32[]{:S(2)}) copy-start(f32[512]{0:T(512)} %param.14) | copy-start | bytes 6148
  98.2 30.6 %copy-start.4 = (s32[1,1,1,256]{3,2,1,0:T(1,128)S(1)}, s32[1,1,1,256]{3,2,1,0:T(1,128)}, u32[]{:S(2)}) copy-start(s32[1,1,1,256]{3,2,1,0:T(1,128)} %param.21) | copy-start | bytes 3076
  100.1 20.1 %all-to-all-start.1 = ((bf16[32,16,512]{2,1,0:T(8,128)(2,1)}), bf16[32,16,512]{2,1,0:T(8,128)(2,1)}, u32[]{:S(2)}, u32[]{:S(2)}) async-start(bf16[32,16,512]{2,1,0:T(8,128)(2,1)} %bitcast.100), calls=%async_computation.1 | async-start | bytes 1048576 | tf_op jit(solution)/shard_map/all_to_all | solution.py:55
  123.7 16.2 %all-to-all-start.2 = ((bf16[32,16,512]{2,1,0:T(8,128)(2,1)}), bf16[32,16,512]{2,1,0:T(8,128)(2,1)}, u32[]{:S(2)}, u32[]{:S(2)}) async-start(bf16[32,16,512]{2,1,0:T(8,128)(2,1)} %broadcast_in_dim.17), calls=%async_computation.2 | async-start | bytes 1048576 | tf_op jit(solution)/shard_map/all_to_all | solution.py:61
  142.0 45.7 %all-to-all-start.3 = ((bf16[32,8,512]{2,1,0:T(8,128)(2,1)}), bf16[32,8,512]{2,1,0:T(8,128)(2,1)S(1)}, u32[]{:S(2)}, u32[]{:S(2)}) async-start(bf16[32,8,512]{2,1,0:T(8,128)(2,1)} %fusion.24), calls=%async_computation.3 | async-start | bytes 524288 | tf_op jit(solution)/shard_map/all_to_all | solution.py:50
  156.4 51.8 %copy-start.6 = (f32[512]{0:T(512)S(1)}, f32[512]{0:T(512)}, u32[]{:S(2)}) copy-start(f32[512]{0:T(512)} %param.17) | copy-start | bytes 6148
  187.7 20.5 %copy-start.3 = (bf16[512,512]{1,0:T(8,128)(2,1)S(1)}, bf16[512,512]{1,0:T(8,128)(2,1)}, u32[]{:S(2)}) copy-start(bf16[512,512]{1,0:T(8,128)(2,1)} %param.16) | copy-start | bytes 1572868

commit v7 on v5

--- a/solution.py
+++ b/solution.py
@@ -33,7 +33,7 @@
     blocks = remote_dense.shape[3]
     rows = far_proj.reshape(blocks, far_proj.shape[0] // blocks, far_proj.shape[1], far_proj.shape[2])
     summed = jnp.einsum("rkasb,sbrh->kah", remote_dense, rows.astype(jnp.float32),
-                        precision=lax.Precision.HIGHEST, preferred_element_type=jnp.float32)
+                        precision=lax.Precision.HIGH, preferred_element_type=jnp.float32)
     return summed.reshape(-1, summed.shape[-1])
 
 
@@ -99,14 +99,14 @@
     first_part = layer_part(features, received, first_weight, local_tiles, remote_dense, local_pick)
     first_share = scatter_sum(first_part.astype(jnp.bfloat16), parts)
     own_features = lax.dynamic_slice_in_dim(features, row_start, share_rows, 0)
-    first_term = jnp.dot(own_features, first_root, preferred_element_type=jnp.float32)
-    hidden_share = jax.nn.relu(first_share + first_term + first_bias).astype(jnp.bfloat16)
+    first_term = lax.optimization_barrier(jnp.dot(own_features, first_root, preferred_element_type=jnp.float32) + first_bias)
+    hidden_share = jax.nn.relu(first_share + first_term).astype(jnp.bfloat16)
     hidden = gather_all(hidden_share, parts)
     received_hidden = fetch_rows(hidden, send_index)
     second_part = layer_part(hidden, received_hidden, second_weight, local_tiles, remote_dense, local_pick)
     second_share = scatter_sum(second_part.astype(jnp.bfloat16), parts)
-    second_term = jnp.dot(hidden_share, second_root, preferred_element_type=jnp.float32)
-    result = jax.nn.relu(second_share + second_term + second_bias).astype(jnp.bfloat16)
+    second_term = lax.optimization_barrier(jnp.dot(hidden_share, second_root, preferred_element_type=jnp.float32) + second_bias)
+    result = jax.nn.relu(second_share + second_term).astype(jnp.bfloat16)
     return result[None]
 
 

time: 208 us -> 207 us (level)
  blocking collectives: 32 us -> 15.5 us
  waiting for transfers between devices: 94.4 us -> 103 us
  starting transfers between devices: 41.9 us -> 47.3 us
    all_to_all x1 -> x0, blocking collectives: 16.5 us -> none  [scatter_sum(): received = lax.all_to_all(chunks, GROUP, 0, 0, tiled=False)]
    all_to_all x1 -> x2, waiting for transfers between devices: 11.5 us -> 20.3 us  [scatter_sum(): received = lax.all_to_all(chunks, GROUP, 0, 0, tiled=False)]
    all_to_all x1 -> x2, starting transfers between devices: 8.61 us -> 14 us  [scatter_sum(): received = lax.all_to_all(chunks, GROUP, 0, 0, tiled=False)]
  transfers between devices with their start and end apart: 3 -> 4, of which waited for: 3 -> 4; matrix products, arithmetic and copies ran while one was open for 11% -> 13% of each run, Pallas kernels for 0% -> 0%
where the time goes in v7:
time: 207 us; the launch traced here: 206 us
  waiting for transfers between devices  103 us (50%)
  starting transfers between devices  47.3 us (23%)
  matrix products  27.1 us (13%)
  blocking collectives  15.5 us (7%)
  local copies, waits for them, and re-layouts  7.5 us (4%)
  other arithmetic  5.43 us (3%)
    all_to_all x2, waiting for transfers between devices, fetch_rows(): lax.all_to_all(outgoing, 'vrow', split_axis=0, concat_axis=0, tiled=True)  83 us
    all_to_all x2, starting transfers between devices, fetch_rows(): lax.all_to_all(outgoing, 'vrow', split_axis=0, concat_axis=0, tiled=True)  33.3 us
    all_to_all x2, waiting for transfers between devices, scatter_sum(): received = lax.all_to_all(chunks, GROUP, 0, 0, tiled=False)  20.3 us
    all_to_all x1, blocking collectives, gather_all(): received = lax.all_to_all(copies, GROUP, 0, 0, tiled=False)  15.5 us
    all_to_all x2, starting transfers between devices, scatter_sum(): received = lax.all_to_all(chunks, GROUP, 0, 0, tiled=False)  14 us
    dot_general x4, matrix products, project(): jnp.einsum('nf,sfh->nsh', row_values, weight, preferred_element_type=jnp....  9.06 us
    dot_general x2, matrix products, aggregate(): jnp.einsum('sktab,sktbh->kah', weighted, picked, preferred_element_type=j...  6.55 us
    gather x4, local copies, waits for them, and re-layouts, pick(): return source_blocks[indices]  6.3 us
  transfers between devices with their start and end apart: 4, of which 4 were waited for; matrix products, arithmetic and copies ran while one was open for 13% of the time, Pallas kernels for 0%

profile of v7, /device:TPU:1, one launch (start us, length us, event | category | flops | bytes accessed | tf_op | source)
XLA Modules:
  0.0 206.2 jit_solution(2205084496331500216)
XLA Ops:
  0.0 0.0 copy-start
  0.0 2.7 %fusion.4 = bf16[32,8,1024]{2,1,0:T(8,128)(2,1)} fusion(bf16[512,1024]{1,0:T(8,128)(2,1)} %param.11, s32[256]{0:T(256)} %bitcast.104), kind=kOutput, calls=%fused_computation.13 | convolution fusion | flops 268828672 | bytes 1573888 | tf_op jit(solution)/shard_map/dot_general | solution.py:49
  2.7 29.4 %all-to-all-start = ((bf16[32,8,1024]{2,1,0:T(8,128)(2,1)}), bf16[32,8,1024]{2,1,0:T(8,128)(2,1)}, u32[]{:S(2)}, u32[]{:S(2)}) async-start(bf16[32,8,1024]{2,1,0:T(8,128)(2,1)} %fusion.4), calls=%async_computation | async-start | bytes 1048576 | tf_op jit(solution)/shard_map/all_to_all | solution.py:50
  32.1 0.7 not_convert_fusion
  32.8 0.1 copy.21
  32.9 0.7 fusion.35
  33.6 0.1 copy.22
  33.7 0.1 reshape.55
  33.8 0.1 copy.26
  33.9 0.7 add_select_fusion
  34.6 0.1 copy.25
  34.7 0.0 copy-done
  34.7 2.5 %convolution_convert_fusion = bf16[512,2,512]{2,0,1:T(8,128)(2,1)S(1)} fusion(bf16[2,1024,512]{2,1,0:T(8,128)(2,1)S(1)} %copy-done, bf16[512,1024]{1,0:T(8,128)(2,1)} %param.11), kind=kOutput, calls=%fused_computation.2 | convolution fusion | flops 1074266112 | bytes 4194304 | tf_op jit(solution)/shard_map/nf,sfh->nsh/dot_general | solution.py:11
  37.2 0.0 copy-start.7
  37.2 2.4 %gather_fusion = bf16[24,128,512]{2,1,0:T(8,128)(2,1)} fusion(bf16[2,4,128,512]{3,2,1,0:T(8,128)(2,1)S(1)} %bitcast.95, s32[24]{0:T(128)S(1)} %reshape.55), kind=kCustom, calls=%fused_computation | custom fusion | bytes 6291648 | tf_op jit(solution)/shard_map/vmap()/gather | solution.py:21
  39.6 0.0 copy-done.7
  39.6 0.1 fusion.31
  39.7 1.4 multiply_multiply_fusion
  41.1 0.8 fusion.7
  41.9 0.0 copy-done.1
  41.9 2.8 %fusion.13 = f32[4,128,512,1,1]{2,1,4,0,3:T(8,128)} fusion(bf16[2,4,3,128,512]{4,3,2,1,0:T(8,128)(2,1)S(1)} %bitcast.90, bf16[2,4,3,128,128]{4,3,2,1,0:T(8,128)(2,1)} %param.18, bf16[2,4,3]{2,1,0:T(4,128)(2,1)S(1)} %copy.21, bf16[2,4,3]{2,1,0:T(4,128)(2,1)S(1)} %fusion.31), kind=kOutput, calls=%fused_computation.27 | convolution fusion | flops 403439616 | bytes 4980832 | tf_op jit(solution)/shard_map/sktab,sktbh->kah/dot_general | solution.py:28
  44.7 51.7 %all-to-all-done = bf16[32,8,1024]{2,1,0:T(8,128)(2,1)} async-done(((bf16[32,8,1024]{2,1,0:T(8,128)(2,1)}), bf16[32,8,1024]{2,1,0:T(8,128)(2,1)}, u32[]{:S(2)}, u32[]{:S(2)}) %all-to-all-start) | async-done | bytes 524320 | tf_op jit(solution)/shard_map/all_to_all | solution.py:50
  96.4 1.8 convolution_convert_fusion.4
  98.2 0.0 copy-done.2
  98.2 0.0 copy-start.4
  98.3 1.5 fusion.3
  99.8 8.6 %all-to-all-start.1 = ((bf16[32,16,512]{2,1,0:T(8,128)(2,1)}), bf16[32,16,512]{2,1,0:T(8,128)(2,1)}, u32[]{:S(2)}, u32[]{:S(2)}) async-start(bf16[32,16,512]{2,1,0:T(8,128)(2,1)} %bitcast.101), calls=%async_computation.1 | async-start | bytes 1048576 | tf_op jit(solution)/shard_map/all_to_all | solution.py:55
  108.4 0.0 copy-done.5
  108.4 1.5 convolution_add_fusion
  109.9 10.0 %all-to-all-done.1 = bf16[32,16,512]{2,1,0:T(8,128)(2,1)} async-done(((bf16[32,16,512]{2,1,0:T(8,128)(2,1)}), bf16[32,16,512]{2,1,0:T(8,128)(2,1)}, u32[]{:S(2)}, u32[]{:S(2)}) %all-to-all-start.1) | async-done | bytes 524320 | tf_op jit(solution)/shard_map/all_to_all | solution.py:55
  119.9 1.1 convert_reduce_fusion.1
  121.0 0.1 broadcast_in_dim.17
  121.1 15.5 %all_to_all.39 = bf16[32,16,512]{2,1,0:T(8,128)(2,1)S(1)} all-to-all(bf16[32,16,512]{2,1,0:T(8,128)(2,1)S(1)} %broadcast_in_dim.17), channel_id=1, replica_groups=mesh['rel'=8,'vrow'=32,'vcol'=4] {'rel','vcol'}, dimensions={0} | all-to-all | bytes 1048576 | tf_op jit(solution)/shard_map/all_to_all | solution.py:61
  136.6 0.8 copy-done.3
  137.4 1.1 fusion.5
  138.4 3.9 %all-to-all-start.3 = ((bf16[32,8,512]{2,1,0:T(8,128)(2,1)}), bf16[32,8,512]{2,1,0:T(8,128)(2,1)S(1)}, u32[]{:S(2)}, u32[]{:S(2)}) async-start(bf16[32,8,512]{2,1,0:T(8,128)(2,1)} %fusion.5), calls=%async_computation.3 | async-start | bytes 524288 | tf_op jit(solution)/shard_map/all_to_all | solution.py:50
  142.3 3.1 %convolution_convert_fusion.1 = bf16[512,2,512]{2,0,1:T(8,128)(2,1)} fusion(bf16[512,512,1]{1,0,2:T(8,128)(2,1)} %bitcast.99, bf16[2,512,512]{2,1,0:T(8,128)(2,1)} %param.15), kind=kOutput, calls=%fused_computation.3 | convolution fusion | flops 537395200 | bytes 2621440 | tf_op jit(solution)/shard_map/nf,sfh->nsh/dot_general | solution.py:11
  145.4 3.7 %gather_fusion.1 = bf16[24,128,512]{2,1,0:T(8,128)(2,1)} fusion(bf16[2,4,128,512]{3,2,1,0:T(8,128)(2,1)} %bitcast.94, s32[24]{0:T(128)S(1)} %reshape.55), kind=kCustom, calls=%fused_computation.1 | custom fusion | bytes 6291648 | tf_op jit(solution)/shard_map/vmap()/gather | solution.py:21
  149.1 3.8 %fusion.11 = f32[4,128,512,1,1]{2,1,4,0,3:T(8,128)} fusion(bf16[2,4,3,128,512]{4,3,2,1,0:T(8,128)(2,1)} %bitcast.91, bf16[2,4,3,128,128]{4,3,2,1,0:T(8,128)(2,1)} %param.18, bf16[2,4,3]{2,1,0:T(4,128)(2,1)S(1)} %copy.21, bf16[2,4,3]{2,1,0:T(4,128)(2,1)S(1)} %fusion.31), kind=kOutput, calls=%fused_computation.25 | convolution fusion | flops 403439616 | bytes 4980832 | tf_op jit(solution)/shard_map/sktab,sktbh->kah/dot_general | solution.py:28
  152.9 31.3 %all-to-all-done.3 = bf16[32,8,512]{2,1,0:T(8,128)(2,1)S(1)} async-done(((bf16[32,8,512]{2,1,0:T(8,128)(2,1)}), bf16[32,8,512]{2,1,0:T(8,128)(2,1)S(1)}, u32[]{:S(2)}, u32[]{:S(2)}) %all-to-all-start.3) | async-done | bytes 262176 | tf_op jit(solution)/shard_map/all_to_all | solution.py:50
  184.1 1.7 convolution_convert_fusion.2
  185.8 2.7 %fusion.2 = bf16[512,512]{1,0:T(8,128)(2,1)} fusion(f32[512,512]{1,0:T(8,128)} %bitcast.96, bf16[2,128,2,512]{3,1,0,2:T(8,128)(2,1)S(1)} %bitcast.100, f32[512,128,2,2]{1,3,0,2:T(2,128)S(1)} %bitcast.93), kind=kOutput, calls=%fused_computation.8 | convolution fusion | flops 805830656 | bytes 3145728 | tf_op jit(solution)/shard_map/rkasb,sbrh->kah/dot_general | solution.py:35
  188.5 5.4 %all-to-all-start.4 = ((bf16[32,16,512]{2,1,0:T(8,128)(2,1)}), bf16[32,16,512]{2,1,0:T(8,128)(2,1)S(1)}, u32[]{:S(2)}, u32[]{:S(2)}) async-start(bf16[32,16,512]{2,1,0:T(8,128)(2,1)} %bitcast.102), calls=%async_computation.4 | async-start | bytes 1048576 | tf_op jit(solution)/shard_map/all_to_all | solution.py:55
  194.0 0.0 copy-done.6
  194.0 1.2 convolution_add_fusion.1
  195.2 10.3 %all-to-all-done.4 = bf16[32,16,512]{2,1,0:T(8,128)(2,1)S(1)} async-done(((bf16[32,16,512]{2,1,0:T(8,128)(2,1)}), bf16[32,16,512]{2,1,0:T(8,128)(2,1)S(1)}, u32[]{:S(2)}, u32[]{:S(2)}) %all-to-all-start.4) | async-done | bytes 524320 | tf_op jit(solution)/shard_map/all_to_all | solution.py:55
  205.5 0.1 convert_reduce_fusion
  205.6 0.6 fusion.26
  (7 shorter events, 0.0 us)
Async XLA Ops:
  0.0 34.7 %copy-start = (bf16[2,1024,512]{2,1,0:T(8,128)(2,1)S(1)}, bf16[2,1024,512]{2,1,0:T(8,128)(2,1)}, u32[]{:S(2)}) copy-start(bf16[2,1024,512]{2,1,0:T(8,128)(2,1)} %param.12) | copy-start | bytes 6291460
  2.7 93.7 %all-to-all-start = ((bf16[32,8,1024]{2,1,0:T(8,128)(2,1)}), bf16[32,8,1024]{2,1,0:T(8,128)(2,1)}, u32[]{:S(2)}, u32[]{:S(2)}) async-start(bf16[32,8,1024]{2,1,0:T(8,128)(2,1)} %fusion.4), calls=%async_computation | async-start | bytes 1048576 | tf_op jit(solution)/shard_map/all_to_all | solution.py:50
  37.2 2.5 %copy-start.7 = (s32[2,4,1]{1,2,0:T(1,128)S(1)}, s32[2,4,1]{1,2,0:T(1,128)}, u32[]{:S(2)}) copy-start(s32[2,4,1]{1,2,0:T(1,128)} %param.20) | copy-start | bytes 100
  39.6 2.3 %copy-start.1 = (bf16[24,128,512]{2,1,0:T(8,128)(2,1)S(1)}, bf16[24,128,512]{2,1,0:T(8,128)(2,1)}, u32[]{:S(2)}) copy-start(bf16[24,128,512]{2,1,0:T(8,128)(2,1)} %gather_fusion) | copy-start | bytes 9437188
  44.7 63.7 %copy-start.5 = (f32[512]{0:T(512)S(1)}, f32[512]{0:T(512)}, u32[]{:S(2)}) copy-start(f32[512]{0:T(512)} %param.14) | copy-start | bytes 6148
  96.4 1.8 copy-start.2
  98.2 39.1 %copy-start.4 = (s32[1,1,1,256]{3,2,1,0:T(1,128)S(1)}, s32[1,1,1,256]{3,2,1,0:T(1,128)}, u32[]{:S(2)}) copy-start(s32[1,1,1,256]{3,2,1,0:T(1,128)} %param.21) | copy-start | bytes 3076
  99.8 20.1 %all-to-all-start.1 = ((bf16[32,16,512]{2,1,0:T(8,128)(2,1)}), bf16[32,16,512]{2,1,0:T(8,128)(2,1)}, u32[]{:S(2)}, u32[]{:S(2)}) async-start(bf16[32,16,512]{2,1,0:T(8,128)(2,1)} %bitcast.101), calls=%async_computation.1 | async-start | bytes 1048576 | tf_op jit(solution)/shard_map/all_to_all | solution.py:55
  136.6 0.8 copy-start.3
  138.4 45.7 %all-to-all-start.3 = ((bf16[32,8,512]{2,1,0:T(8,128)(2,1)}), bf16[32,8,512]{2,1,0:T(8,128)(2,1)S(1)}, u32[]{:S(2)}, u32[]{:S(2)}) async-start(bf16[32,8,512]{2,1,0:T(8,128)(2,1)} %fusion.5), calls=%async_computation.3 | async-start | bytes 524288 | tf_op jit(solution)/shard_map/all_to_all | solution.py:50
  152.9 41.1 %copy-start.6 = (f32[512]{0:T(512)S(1)}, f32[512]{0:T(512)}, u32[]{:S(2)}) copy-start(f32[512]{0:T(512)} %param.17) | copy-start | bytes 6148
  188.5 16.9 %all-to-all-start.4 = ((bf16[32,16,512]{2,1,0:T(8,128)(2,1)}), bf16[32,16,512]{2,1,0:T(8,128)(2,1)S(1)}, u32[]{:S(2)}, u32[]{:S(2)}) async-start(bf16[32,16,512]{2,1,0:T(8,128)(2,1)} %bitcast.102), calls=%async_computation.4 | async-start | bytes 1048576 | tf_op jit(solution)/shard_map/all_to_all | solution.py:55

commit v8 on v7

--- a/solution.py
+++ b/solution.py
@@ -44,9 +44,8 @@
     return own_sum + far_aggregate(far_proj, remote_dense)
 
 
-def fetch_rows(values, send_index):
-    chooser = (send_index[:, None] == jnp.arange(values.shape[0], dtype=send_index.dtype)[None, :])
-    outgoing = jnp.dot(chooser.astype(values.dtype), values, preferred_element_type=jnp.float32).astype(values.dtype)
+def fetch_rows(values, chooser):
+    outgoing = jnp.dot(chooser, values, preferred_element_type=jnp.float32).astype(values.dtype)
     return lax.all_to_all(outgoing, "vrow", split_axis=0, concat_axis=0, tiled=True)
 
 
@@ -95,14 +94,16 @@
     parts = lax.axis_size(GROUP)
     share_rows = local_rows // parts
     row_start = lax.axis_index(GROUP) * share_rows
-    received = fetch_rows(features, send_index)
+    chooser = send_index[:, None] == jnp.arange(local_rows, dtype=send_index.dtype)[None, :]
+    chooser = lax.optimization_barrier(chooser.astype(features.dtype))
+    received = fetch_rows(features, chooser)
     first_part = layer_part(features, received, first_weight, local_tiles, remote_dense, local_pick)
     first_share = scatter_sum(first_part.astype(jnp.bfloat16), parts)
     own_features = lax.dynamic_slice_in_dim(features, row_start, share_rows, 0)
     first_term = lax.optimization_barrier(jnp.dot(own_features, first_root, preferred_element_type=jnp.float32) + first_bias)
     hidden_share = jax.nn.relu(first_share + first_term).astype(jnp.bfloat16)
     hidden = gather_all(hidden_share, parts)
-    received_hidden = fetch_rows(hidden, send_index)
+    received_hidden = fetch_rows(hidden, chooser)
     second_part = layer_part(hidden, received_hidden, second_weight, local_tiles, remote_dense, local_pick)
     second_share = scatter_sum(second_part.astype(jnp.bfloat16), parts)
     second_term = lax.optimization_barrier(jnp.dot(hidden_share, second_root, preferred_element_type=jnp.float32) + second_bias)

time: 207 us -> 208 us (level)
  transfers between devices with their start and end apart: 4 -> 4, of which waited for: 4 -> 4; matrix products, arithmetic and copies ran while one was open for 13% -> 11% of each run, Pallas kernels for 0% -> 0%
where the time goes in v8:
time: 208 us; the launch traced here: 207 us
  waiting for transfers between devices  105 us (50%)
  starting transfers between devices  47.3 us (23%)
  matrix products  26.8 us (13%)
  blocking collectives  15.5 us (7%)
  local copies, waits for them, and re-layouts  7.5 us (4%)
  other arithmetic  4.32 us (2%)
    all_to_all x2, waiting for transfers between devices, fetch_rows(): lax.all_to_all(outgoing, 'vrow', split_axis=0, concat_axis=0, tiled=True)  85 us
    all_to_all x2, starting transfers between devices, fetch_rows(): lax.all_to_all(outgoing, 'vrow', split_axis=0, concat_axis=0, tiled=True)  33.3 us
    all_to_all x2, waiting for transfers between devices, scatter_sum(): received = lax.all_to_all(chunks, GROUP, 0, 0, tiled=False)  20.3 us
    all_to_all x1, blocking collectives, gather_all(): received = lax.all_to_all(copies, GROUP, 0, 0, tiled=False)  15.5 us
    all_to_all x2, starting transfers between devices, scatter_sum(): received = lax.all_to_all(chunks, GROUP, 0, 0, tiled=False)  14 us
    dot_general x4, matrix products, project(): jnp.einsum('nf,sfh->nsh', row_values, weight, preferred_element_type=jnp....  9.06 us
    dot_general x2, matrix products, aggregate(): jnp.einsum('sktab,sktbh->kah', weighted, picked, preferred_element_type=j...  6.55 us
    gather x4, local copies, waits for them, and re-layouts, pick(): return source_blocks[indices]  6.3 us
  transfers between devices with their start and end apart: 4, of which 4 were waited for; matrix products, arithmetic and copies ran while one was open for 11% of the time, Pallas kernels for 0%

profile of v8, /device:TPU:1, one launch (start us, length us, event | category | flops | bytes accessed | tf_op | source)
XLA Modules:
  0.0 206.9 jit_solution(15376083596383465280)
XLA Ops:
  0.0 0.0 copy-start
  0.0 0.0 copy-start.4
  0.0 0.9 fusion.18
  1.0 2.5 %fusion.4 = bf16[32,8,1024]{2,1,0:T(8,128)(2,1)} fusion(bf16[256,512]{1,0:T(8,128)(2,1)S(1)} %fusion.18, bf16[512,1024]{1,0:T(8,128)(2,1)} %param.11), kind=kOutput, calls=%fused_computation.13 | convolution fusion | flops 268697600 | bytes 1835008 | tf_op jit(solution)/shard_map/dot_general | solution.py:48
  3.4 29.4 %all-to-all-start = ((bf16[32,8,1024]{2,1,0:T(8,128)(2,1)}), bf16[32,8,1024]{2,1,0:T(8,128)(2,1)}, u32[]{:S(2)}, u32[]{:S(2)}) async-start(bf16[32,8,1024]{2,1,0:T(8,128)(2,1)} %fusion.4), calls=%async_computation | async-start | bytes 1048576 | tf_op jit(solution)/shard_map/all_to_all | solution.py:49
  32.8 0.0 copy-done.4
  32.9 0.1 copy.21
  33.0 0.1 copy.22
  33.1 0.1 reshape.55
  33.2 0.1 copy.26
  33.3 0.1 copy.25
  33.4 0.0 copy-done
  33.4 2.5 %convolution_convert_fusion = bf16[512,2,512]{2,0,1:T(8,128)(2,1)S(1)} fusion(bf16[2,1024,512]{2,1,0:T(8,128)(2,1)S(1)} %copy-done, bf16[512,1024]{1,0:T(8,128)(2,1)} %param.11), kind=kOutput, calls=%fused_computation.2 | convolution fusion | flops 1074266112 | bytes 4194304 | tf_op jit(solution)/shard_map/nf,sfh->nsh/dot_general | solution.py:11
  35.9 0.0 copy-start.7
  35.9 2.4 %gather_fusion = bf16[24,128,512]{2,1,0:T(8,128)(2,1)} fusion(bf16[2,4,128,512]{3,2,1,0:T(8,128)(2,1)S(1)} %bitcast.97, s32[24]{0:T(128)S(1)} %reshape.55), kind=kCustom, calls=%fused_computation | custom fusion | bytes 6291648 | tf_op jit(solution)/shard_map/vmap()/gather | solution.py:21
  38.3 0.0 copy-start.1
  38.3 0.0 copy-done.7
  38.3 0.1 fusion.30
  38.4 1.4 multiply_multiply_fusion
  39.9 0.8 fusion.7
  40.6 0.0 copy-done.1
  40.7 2.8 %fusion.13 = f32[4,128,512,1,1]{2,1,4,0,3:T(8,128)} fusion(bf16[2,4,3,128,512]{4,3,2,1,0:T(8,128)(2,1)S(1)} %bitcast.92, bf16[2,4,3,128,128]{4,3,2,1,0:T(8,128)(2,1)} %param.18, bf16[2,4,3]{2,1,0:T(4,128)(2,1)S(1)} %copy.21, bf16[2,4,3]{2,1,0:T(4,128)(2,1)S(1)} %fusion.30), kind=kOutput, calls=%fused_computation.27 | convolution fusion | flops 403439616 | bytes 4980832 | tf_op jit(solution)/shard_map/sktab,sktbh->kah/dot_general | solution.py:28
  43.4 53.7 %all-to-all-done = bf16[32,8,1024]{2,1,0:T(8,128)(2,1)} async-done(((bf16[32,8,1024]{2,1,0:T(8,128)(2,1)}), bf16[32,8,1024]{2,1,0:T(8,128)(2,1)}, u32[]{:S(2)}, u32[]{:S(2)}) %all-to-all-start) | async-done | bytes 524320 | tf_op jit(solution)/shard_map/all_to_all | solution.py:49
  97.1 1.8 convolution_convert_fusion.4
  99.0 0.0 copy-done.2
  99.0 1.5 fusion.3
  100.5 8.6 %all-to-all-start.1 = ((bf16[32,16,512]{2,1,0:T(8,128)(2,1)}), bf16[32,16,512]{2,1,0:T(8,128)(2,1)}, u32[]{:S(2)}, u32[]{:S(2)}) async-start(bf16[32,16,512]{2,1,0:T(8,128)(2,1)} %bitcast.103), calls=%async_computation.1 | async-start | bytes 1048576 | tf_op jit(solution)/shard_map/all_to_all | solution.py:54
  109.1 0.0 copy-done.5
  109.1 1.5 convolution_add_fusion
  110.6 10.0 %all-to-all-done.1 = bf16[32,16,512]{2,1,0:T(8,128)(2,1)} async-done(((bf16[32,16,512]{2,1,0:T(8,128)(2,1)}), bf16[32,16,512]{2,1,0:T(8,128)(2,1)}, u32[]{:S(2)}, u32[]{:S(2)}) %all-to-all-start.1) | async-done | bytes 524320 | tf_op jit(solution)/shard_map/all_to_all | solution.py:54
  120.6 1.1 convert_reduce_fusion.1
  121.7 0.1 broadcast_in_dim.17
  121.8 15.5 %all_to_all.39 = bf16[32,16,512]{2,1,0:T(8,128)(2,1)S(1)} all-to-all(bf16[32,16,512]{2,1,0:T(8,128)(2,1)S(1)} %broadcast_in_dim.17), channel_id=1, replica_groups=mesh['rel'=8,'vrow'=32,'vcol'=4] {'rel','vcol'}, dimensions={0} | all-to-all | bytes 1048576 | tf_op jit(solution)/shard_map/all_to_all | solution.py:60
  137.3 0.8 copy-done.3
  138.1 1.0 fusion.5
  139.1 3.9 %all-to-all-start.3 = ((bf16[32,8,512]{2,1,0:T(8,128)(2,1)}), bf16[32,8,512]{2,1,0:T(8,128)(2,1)S(1)}, u32[]{:S(2)}, u32[]{:S(2)}) async-start(bf16[32,8,512]{2,1,0:T(8,128)(2,1)} %fusion.5), calls=%async_computation.3 | async-start | bytes 524288 | tf_op jit(solution)/shard_map/all_to_all | solution.py:49
  143.0 3.1 %convolution_convert_fusion.1 = bf16[512,2,512]{2,0,1:T(8,128)(2,1)} fusion(bf16[512,512,1]{1,0,2:T(8,128)(2,1)} %bitcast.101, bf16[2,512,512]{2,1,0:T(8,128)(2,1)} %param.15), kind=kOutput, calls=%fused_computation.3 | convolution fusion | flops 537395200 | bytes 2621440 | tf_op jit(solution)/shard_map/nf,sfh->nsh/dot_general | solution.py:11
  146.1 3.7 %gather_fusion.1 = bf16[24,128,512]{2,1,0:T(8,128)(2,1)} fusion(bf16[2,4,128,512]{3,2,1,0:T(8,128)(2,1)} %bitcast.96, s32[24]{0:T(128)S(1)} %reshape.55), kind=kCustom, calls=%fused_computation.1 | custom fusion | bytes 6291648 | tf_op jit(solution)/shard_map/vmap()/gather | solution.py:21
  149.8 3.8 %fusion.11 = f32[4,128,512,1,1]{2,1,4,0,3:T(8,128)} fusion(bf16[2,4,3,128,512]{4,3,2,1,0:T(8,128)(2,1)} %bitcast.93, bf16[2,4,3,128,128]{4,3,2,1,0:T(8,128)(2,1)} %param.18, bf16[2,4,3]{2,1,0:T(4,128)(2,1)S(1)} %copy.21, bf16[2,4,3]{2,1,0:T(4,128)(2,1)S(1)} %fusion.30), kind=kOutput, calls=%fused_computation.25 | convolution fusion | flops 403439616 | bytes 4980832 | tf_op jit(solution)/shard_map/sktab,sktbh->kah/dot_general | solution.py:28
  153.6 31.3 %all-to-all-done.3 = bf16[32,8,512]{2,1,0:T(8,128)(2,1)S(1)} async-done(((bf16[32,8,512]{2,1,0:T(8,128)(2,1)}), bf16[32,8,512]{2,1,0:T(8,128)(2,1)S(1)}, u32[]{:S(2)}, u32[]{:S(2)}) %all-to-all-start.3) | async-done | bytes 262176 | tf_op jit(solution)/shard_map/all_to_all | solution.py:49
  184.8 1.7 convolution_convert_fusion.2
  186.5 2.7 %fusion.2 = bf16[512,512]{1,0:T(8,128)(2,1)} fusion(f32[512,512]{1,0:T(8,128)} %bitcast.98, bf16[2,128,2,512]{3,1,0,2:T(8,128)(2,1)S(1)} %bitcast.102, f32[512,128,2,2]{1,3,0,2:T(2,128)S(1)} %bitcast.95), kind=kOutput, calls=%fused_computation.8 | convolution fusion | flops 805830656 | bytes 3145728 | tf_op jit(solution)/shard_map/rkasb,sbrh->kah/dot_general | solution.py:35
  189.2 5.4 %all-to-all-start.4 = ((bf16[32,16,512]{2,1,0:T(8,128)(2,1)}), bf16[32,16,512]{2,1,0:T(8,128)(2,1)S(1)}, u32[]{:S(2)}, u32[]{:S(2)}) async-start(bf16[32,16,512]{2,1,0:T(8,128)(2,1)} %bitcast.104), calls=%async_computation.4 | async-start | bytes 1048576 | tf_op jit(solution)/shard_map/all_to_all | solution.py:54
  194.7 0.0 copy-done.6
  194.7 1.2 convolution_add_fusion.1
  195.9 10.3 %all-to-all-done.4 = bf16[32,16,512]{2,1,0:T(8,128)(2,1)S(1)} async-done(((bf16[32,16,512]{2,1,0:T(8,128)(2,1)}), bf16[32,16,512]{2,1,0:T(8,128)(2,1)S(1)}, u32[]{:S(2)}, u32[]{:S(2)}) %all-to-all-start.4) | async-done | bytes 524320 | tf_op jit(solution)/shard_map/all_to_all | solution.py:54
  206.2 0.1 convert_reduce_fusion
  206.3 0.6 fusion.25
  (8 shorter events, 0.0 us)
Async XLA Ops:
  0.0 33.4 %copy-start = (bf16[2,1024,512]{2,1,0:T(8,128)(2,1)S(1)}, bf16[2,1024,512]{2,1,0:T(8,128)(2,1)}, u32[]{:S(2)}) copy-start(bf16[2,1024,512]{2,1,0:T(8,128)(2,1)} %param.12) | copy-start | bytes 6291460
  0.0 32.8 %copy-start.4 = (s32[2,4,3]{1,0,2:T(2,128)S(1)}, s32[2,4,3]{1,0,2:T(2,128)}, u32[]{:S(2)}) copy-start(s32[2,4,3]{1,0,2:T(2,128)} %param.19) | copy-start | bytes 292
  3.4 93.7 %all-to-all-start = ((bf16[32,8,1024]{2,1,0:T(8,128)(2,1)}), bf16[32,8,1024]{2,1,0:T(8,128)(2,1)}, u32[]{:S(2)}, u32[]{:S(2)}) async-start(bf16[32,8,1024]{2,1,0:T(8,128)(2,1)} %fusion.4), calls=%async_computation | async-start | bytes 1048576 | tf_op jit(solution)/shard_map/all_to_all | solution.py:49
  35.9 2.5 %copy-start.7 = (s32[2,4,1]{1,2,0:T(1,128)S(1)}, s32[2,4,1]{1,2,0:T(1,128)}, u32[]{:S(2)}) copy-start(s32[2,4,1]{1,2,0:T(1,128)} %param.20) | copy-start | bytes 100
  38.3 2.3 %copy-start.1 = (bf16[24,128,512]{2,1,0:T(8,128)(2,1)S(1)}, bf16[24,128,512]{2,1,0:T(8,128)(2,1)}, u32[]{:S(2)}) copy-start(bf16[24,128,512]{2,1,0:T(8,128)(2,1)} %gather_fusion) | copy-start | bytes 9437188
  43.4 65.7 %copy-start.5 = (f32[512]{0:T(512)S(1)}, f32[512]{0:T(512)}, u32[]{:S(2)}) copy-start(f32[512]{0:T(512)} %param.14) | copy-start | bytes 6148
  97.1 1.8 copy-start.2
  100.5 20.1 %all-to-all-start.1 = ((bf16[32,16,512]{2,1,0:T(8,128)(2,1)}), bf16[32,16,512]{2,1,0:T(8,128)(2,1)}, u32[]{:S(2)}, u32[]{:S(2)}) async-start(bf16[32,16,512]{2,1,0:T(8,128)(2,1)} %bitcast.103), calls=%async_computation.1 | async-start | bytes 1048576 | tf_op jit(solution)/shard_map/all_to_all | solution.py:54
  137.3 0.8 copy-start.3
  139.1 45.7 %all-to-all-start.3 = ((bf16[32,8,512]{2,1,0:T(8,128)(2,1)}), bf16[32,8,512]{2,1,0:T(8,128)(2,1)S(1)}, u32[]{:S(2)}, u32[]{:S(2)}) async-start(bf16[32,8,512]{2,1,0:T(8,128)(2,1)} %fusion.5), calls=%async_computation.3 | async-start | bytes 524288 | tf_op jit(solution)/shard_map/all_to_all | solution.py:49
  153.6 41.1 %copy-start.6 = (f32[512]{0:T(512)S(1)}, f32[512]{0:T(512)}, u32[]{:S(2)}) copy-start(f32[512]{0:T(512)} %param.17) | copy-start | bytes 6148
  189.2 16.9 %all-to-all-start.4 = ((bf16[32,16,512]{2,1,0:T(8,128)(2,1)}), bf16[32,16,512]{2,1,0:T(8,128)(2,1)S(1)}, u32[]{:S(2)}, u32[]{:S(2)}) async-start(bf16[32,16,512]{2,1,0:T(8,128)(2,1)} %bitcast.104), calls=%async_computation.4 | async-start | bytes 1048576 | tf_op jit(solution)/shard_map/all_to_all | solution.py:54

commit v9 on v7

--- a/solution.py
+++ b/solution.py
@@ -33,7 +33,7 @@
     blocks = remote_dense.shape[3]
     rows = far_proj.reshape(blocks, far_proj.shape[0] // blocks, far_proj.shape[1], far_proj.shape[2])
     summed = jnp.einsum("rkasb,sbrh->kah", remote_dense, rows.astype(jnp.float32),
-                        precision=lax.Precision.HIGH, preferred_element_type=jnp.float32)
+                        preferred_element_type=jnp.float32)
     return summed.reshape(-1, summed.shape[-1])
 
 

time: 207 us -> 204 us (0.986)
  waiting for transfers between devices: 103 us -> 108 us
  matrix products: 27.1 us -> 23 us
    all_to_all x2, waiting for transfers between devices: 83 us -> 87.5 us  [fetch_rows(): lax.all_to_all(outgoing, 'vrow', split_axis=0, concat_axis=0, tiled=True)]
    dot_general x2, matrix products: 6.55 us -> 3.43 us  [aggregate(): jnp.einsum('sktab,sktbh->kah', weighted, picked, preferred_element_type=j...]
  transfers between devices with their start and end apart: 4 -> 4, of which waited for: 4 -> 4; matrix products, arithmetic and copies ran while one was open for 13% -> 10% of each run, Pallas kernels for 0% -> 0%
where the time goes in v9:
time: 204 us
  waiting for transfers between devices  108 us (53%)
  starting transfers between devices  47.2 us (23%)
  matrix products  23 us (11%)
  blocking collectives  15.5 us (8%)
  local copies, waits for them, and re-layouts  5.5 us (3%)
  other arithmetic  4.38 us (2%)
    all_to_all x2, waiting for transfers between devices, fetch_rows(): lax.all_to_all(outgoing, 'vrow', split_axis=0, concat_axis=0, tiled=True)  87.5 us
    all_to_all x2, starting transfers between devices, fetch_rows(): lax.all_to_all(outgoing, 'vrow', split_axis=0, concat_axis=0, tiled=True)  33.3 us
    all_to_all x2, waiting for transfers between devices, scatter_sum(): received = lax.all_to_all(chunks, GROUP, 0, 0, tiled=False)  20.2 us
    all_to_all x1, blocking collectives, gather_all(): received = lax.all_to_all(copies, GROUP, 0, 0, tiled=False)  15.5 us
    all_to_all x2, starting transfers between devices, scatter_sum(): received = lax.all_to_all(chunks, GROUP, 0, 0, tiled=False)  14 us
    dot_general x4, matrix products, project(): jnp.einsum('nf,sfh->nsh', row_values, weight, preferred_element_type=jnp....  8.02 us
    gather x4, local copies, waits for them, and re-layouts, pick(): return source_blocks[indices]  5.08 us
  transfers between devices with their start and end apart: 4, of which 4 were waited for; matrix products, arithmetic and copies ran while one was open for 10% of the time, Pallas kernels for 0%

profile of v9, /device:TPU:1, one launch (start us, length us, event | category | flops | bytes accessed | tf_op | source)
XLA Modules:
  0.0 203.5 jit_solution(500817737302029573)
XLA Ops:
  0.0 0.0 copy-start
  0.0 2.7 %fusion.4 = bf16[32,8,1024]{2,1,0:T(8,128)(2,1)} fusion(bf16[512,1024]{1,0:T(8,128)(2,1)} %param.11, s32[256]{0:T(256)} %bitcast.104), kind=kOutput, calls=%fused_computation.13 | convolution fusion | flops 268828672 | bytes 1573888 | tf_op jit(solution)/shard_map/dot_general | solution.py:49
  2.7 29.4 %all-to-all-start = ((bf16[32,8,1024]{2,1,0:T(8,128)(2,1)}), bf16[32,8,1024]{2,1,0:T(8,128)(2,1)}, u32[]{:S(2)}, u32[]{:S(2)}) async-start(bf16[32,8,1024]{2,1,0:T(8,128)(2,1)} %fusion.4), calls=%async_computation | async-start | bytes 1048576 | tf_op jit(solution)/shard_map/all_to_all | solution.py:50
  32.1 0.7 not_convert_fusion
  32.8 0.1 copy.21
  32.9 0.7 fusion.35
  33.6 0.1 copy.22
  33.7 0.1 reshape.55
  33.8 0.1 copy.26
  33.9 0.7 add_select_fusion
  34.6 0.1 copy.25
  34.7 0.0 copy-done
  34.7 2.5 %convolution_convert_fusion = bf16[512,2,512]{2,0,1:T(8,128)(2,1)S(1)} fusion(bf16[2,1024,512]{2,1,0:T(8,128)(2,1)S(1)} %copy-done, bf16[512,1024]{1,0:T(8,128)(2,1)} %param.11), kind=kOutput, calls=%fused_computation.2 | convolution fusion | flops 1074266112 | bytes 4194304 | tf_op jit(solution)/shard_map/nf,sfh->nsh/dot_general | solution.py:11
  37.2 0.0 copy-start.8
  37.2 2.4 %gather_fusion = bf16[24,128,512]{2,1,0:T(8,128)(2,1)} fusion(bf16[2,4,128,512]{3,2,1,0:T(8,128)(2,1)S(1)} %bitcast.93, s32[24]{0:T(128)S(1)} %reshape.55), kind=kCustom, calls=%fused_computation | custom fusion | bytes 6291648 | tf_op jit(solution)/shard_map/vmap()/gather | solution.py:21
  39.6 0.0 copy-done.8
  39.6 0.1 fusion.31
  39.7 1.4 multiply_multiply_fusion
  41.1 1.6 fusion.7
  42.7 0.0 copy-done.1
  42.8 0.7 fusion.13
  43.4 0.0 copy-start.6
  43.4 53.0 %all-to-all-done = bf16[32,8,1024]{2,1,0:T(8,128)(2,1)} async-done(((bf16[32,8,1024]{2,1,0:T(8,128)(2,1)}), bf16[32,8,1024]{2,1,0:T(8,128)(2,1)}, u32[]{:S(2)}, u32[]{:S(2)}) %all-to-all-start) | async-done | bytes 524320 | tf_op jit(solution)/shard_map/all_to_all | solution.py:50
  96.4 1.8 convolution_convert_fusion.4
  98.2 0.0 copy-start.5
  98.2 1.2 fusion.3
  99.5 8.6 %all-to-all-start.1 = ((bf16[32,16,512]{2,1,0:T(8,128)(2,1)}), bf16[32,16,512]{2,1,0:T(8,128)(2,1)S(1)}, u32[]{:S(2)}, u32[]{:S(2)}) async-start(bf16[32,16,512]{2,1,0:T(8,128)(2,1)} %bitcast.99), calls=%async_computation.1 | async-start | bytes 1048576 | tf_op jit(solution)/shard_map/all_to_all | solution.py:55
  108.0 1.5 convolution_add_fusion
  109.5 9.9 %all-to-all-done.1 = bf16[32,16,512]{2,1,0:T(8,128)(2,1)S(1)} async-done(((bf16[32,16,512]{2,1,0:T(8,128)(2,1)}), bf16[32,16,512]{2,1,0:T(8,128)(2,1)S(1)}, u32[]{:S(2)}, u32[]{:S(2)}) %all-to-all-start.1) | async-done | bytes 524320 | tf_op jit(solution)/shard_map/all_to_all | solution.py:55
  119.5 0.1 convert_reduce_fusion.1
  119.6 0.1 broadcast_in_dim.17
  119.6 15.5 %all_to_all.39 = bf16[32,16,512]{2,1,0:T(8,128)(2,1)S(1)} all-to-all(bf16[32,16,512]{2,1,0:T(8,128)(2,1)S(1)} %broadcast_in_dim.17), channel_id=1, replica_groups=mesh['rel'=8,'vrow'=32,'vcol'=4] {'rel','vcol'}, dimensions={0} | all-to-all | bytes 1048576 | tf_op jit(solution)/shard_map/all_to_all | solution.py:61
  135.1 0.0 copy-done.5
  135.1 1.1 fusion.5
  136.2 3.9 %all-to-all-start.3 = ((bf16[32,8,512]{2,1,0:T(8,128)(2,1)}), bf16[32,8,512]{2,1,0:T(8,128)(2,1)S(1)}, u32[]{:S(2)}, u32[]{:S(2)}) async-start(bf16[32,8,512]{2,1,0:T(8,128)(2,1)} %fusion.5), calls=%async_computation.3 | async-start | bytes 524288 | tf_op jit(solution)/shard_map/all_to_all | solution.py:50
  140.1 2.1 %convolution_convert_fusion.1 = bf16[512,2,512]{2,0,1:T(8,128)(2,1)S(1)} fusion(bf16[512,512,1]{1,0,2:T(8,128)(2,1)} %bitcast.102, bf16[2,512,512]{2,1,0:T(8,128)(2,1)} %param.15), kind=kOutput, calls=%fused_computation.3 | convolution fusion | flops 537395200 | bytes 2621440 | tf_op jit(solution)/shard_map/nf,sfh->nsh/dot_general | solution.py:11
  142.2 2.4 %gather_fusion.1 = bf16[24,128,512]{2,1,0:T(8,128)(2,1)} fusion(bf16[2,4,128,512]{3,2,1,0:T(8,128)(2,1)S(1)} %bitcast.92, s32[24]{0:T(128)S(1)} %reshape.55), kind=kCustom, calls=%fused_computation.1 | custom fusion | bytes 6291648 | tf_op jit(solution)/shard_map/vmap()/gather | solution.py:21
  144.7 2.8 %fusion.11 = f32[4,128,512,1,1]{2,1,4,0,3:T(8,128)S(1)} fusion(bf16[2,4,3,128,512]{4,3,2,1,0:T(8,128)(2,1)} %bitcast.91, bf16[2,4,3,128,128]{4,3,2,1,0:T(8,128)(2,1)} %param.18, bf16[2,4,3]{2,1,0:T(4,128)(2,1)S(1)} %copy.21, bf16[2,4,3]{2,1,0:T(4,128)(2,1)S(1)} %fusion.31), kind=kOutput, calls=%fused_computation.25 | convolution fusion | flops 403439616 | bytes 4980832 | tf_op jit(solution)/shard_map/sktab,sktbh->kah/dot_general | solution.py:28
  147.4 0.0 copy-start.7
  147.4 34.5 %all-to-all-done.3 = bf16[32,8,512]{2,1,0:T(8,128)(2,1)S(1)} async-done(((bf16[32,8,512]{2,1,0:T(8,128)(2,1)}), bf16[32,8,512]{2,1,0:T(8,128)(2,1)S(1)}, u32[]{:S(2)}, u32[]{:S(2)}) %all-to-all-start.3) | async-done | bytes 262176 | tf_op jit(solution)/shard_map/all_to_all | solution.py:50
  181.9 1.7 convolution_convert_fusion.2
  183.6 2.3 %fusion.2 = bf16[512,512]{1,0:T(8,128)(2,1)} fusion(f32[512,512]{1,0:T(8,128)S(1)} %bitcast.94, bf16[2,128,2,512]{3,1,0,2:T(8,128)(2,1)S(1)} %bitcast.98, bf16[512,128,2,2]{1,3,0,2:T(2,128)(2,1)} %bitcast.96), kind=kOutput, calls=%fused_computation.8 | convolution fusion | flops 268959744 | bytes 2621440 | tf_op jit(solution)/shard_map/rkasb,sbrh->kah/dot_general | solution.py:35
  185.9 5.4 %all-to-all-start.4 = ((bf16[32,16,512]{2,1,0:T(8,128)(2,1)}), bf16[32,16,512]{2,1,0:T(8,128)(2,1)S(1)}, u32[]{:S(2)}, u32[]{:S(2)}) async-start(bf16[32,16,512]{2,1,0:T(8,128)(2,1)} %bitcast.100), calls=%async_computation.4 | async-start | bytes 1048576 | tf_op jit(solution)/shard_map/all_to_all | solution.py:55
  191.3 0.0 copy-done.7
  191.3 1.2 convolution_add_fusion.1
  192.5 10.3 %all-to-all-done.4 = bf16[32,16,512]{2,1,0:T(8,128)(2,1)S(1)} async-done(((bf16[32,16,512]{2,1,0:T(8,128)(2,1)}), bf16[32,16,512]{2,1,0:T(8,128)(2,1)S(1)}, u32[]{:S(2)}, u32[]{:S(2)}) %all-to-all-start.4) | async-done | bytes 524320 | tf_op jit(solution)/shard_map/all_to_all | solution.py:55
  202.8 0.1 convert_reduce_fusion
  202.9 0.6 fusion.26
  (9 shorter events, 0.0 us)
Async XLA Ops:
  0.0 34.7 %copy-start = (bf16[2,1024,512]{2,1,0:T(8,128)(2,1)S(1)}, bf16[2,1024,512]{2,1,0:T(8,128)(2,1)}, u32[]{:S(2)}) copy-start(bf16[2,1024,512]{2,1,0:T(8,128)(2,1)} %param.12) | copy-start | bytes 6291460
  2.7 93.7 %all-to-all-start = ((bf16[32,8,1024]{2,1,0:T(8,128)(2,1)}), bf16[32,8,1024]{2,1,0:T(8,128)(2,1)}, u32[]{:S(2)}, u32[]{:S(2)}) async-start(bf16[32,8,1024]{2,1,0:T(8,128)(2,1)} %fusion.4), calls=%async_computation | async-start | bytes 1048576 | tf_op jit(solution)/shard_map/all_to_all | solution.py:50
  37.2 2.5 %copy-start.8 = (s32[2,4,1]{1,2,0:T(1,128)S(1)}, s32[2,4,1]{1,2,0:T(1,128)}, u32[]{:S(2)}) copy-start(s32[2,4,1]{1,2,0:T(1,128)} %param.20) | copy-start | bytes 100
  39.6 3.1 %copy-start.1 = (bf16[24,128,512]{2,1,0:T(8,128)(2,1)S(1)}, bf16[24,128,512]{2,1,0:T(8,128)(2,1)}, u32[]{:S(2)}) copy-start(bf16[24,128,512]{2,1,0:T(8,128)(2,1)} %gather_fusion) | copy-start | bytes 9437188
  39.6 3.1 %copy-start.2 = (bf16[2,4,3,128,128]{4,3,2,1,0:T(8,128)(2,1)S(1)}, bf16[2,4,3,128,128]{4,3,2,1,0:T(8,128)(2,1)}, u32[]{:S(2)}) copy-start(bf16[2,4,3,128,128]{4,3,2,1,0:T(8,128)(2,1)} %param.18) | copy-start | bytes 2359300
  43.4 64.6 %copy-start.6 = (f32[512]{0:T(512)S(1)}, f32[512]{0:T(512)}, u32[]{:S(2)}) copy-start(f32[512]{0:T(512)} %param.14) | copy-start | bytes 6148
  96.4 1.8 copy-start.3
  98.2 36.9 %copy-start.5 = (s32[1,1,1,256]{3,2,1,0:T(1,128)S(1)}, s32[1,1,1,256]{3,2,1,0:T(1,128)}, u32[]{:S(2)}) copy-start(s32[1,1,1,256]{3,2,1,0:T(1,128)} %param.21) | copy-start | bytes 3076
  99.5 20.0 %all-to-all-start.1 = ((bf16[32,16,512]{2,1,0:T(8,128)(2,1)}), bf16[32,16,512]{2,1,0:T(8,128)(2,1)S(1)}, u32[]{:S(2)}, u32[]{:S(2)}) async-start(bf16[32,16,512]{2,1,0:T(8,128)(2,1)} %bitcast.99), calls=%async_computation.1 | async-start | bytes 1048576 | tf_op jit(solution)/shard_map/all_to_all | solution.py:55
  135.1 5.0 %copy-start.4 = (bf16[32,16,512]{2,1,0:T(8,128)(2,1)}, bf16[32,16,512]{2,1,0:T(8,128)(2,1)S(1)}, u32[]{:S(2)}) copy-start(bf16[32,16,512]{2,1,0:T(8,128)(2,1)S(1)} %all_to_all.39) | copy-start | bytes 1572868
  136.2 45.7 %all-to-all-start.3 = ((bf16[32,8,512]{2,1,0:T(8,128)(2,1)}), bf16[32,8,512]{2,1,0:T(8,128)(2,1)S(1)}, u32[]{:S(2)}, u32[]{:S(2)}) async-start(bf16[32,8,512]{2,1,0:T(8,128)(2,1)} %fusion.5), calls=%async_computation.3 | async-start | bytes 524288 | tf_op jit(solution)/shard_map/all_to_all | solution.py:50
  147.4 43.9 %copy-start.7 = (f32[512]{0:T(512)S(1)}, f32[512]{0:T(512)}, u32[]{:S(2)}) copy-start(f32[512]{0:T(512)} %param.17) | copy-start | bytes 6148
  185.9 16.9 %all-to-all-start.4 = ((bf16[32,16,512]{2,1,0:T(8,128)(2,1)}), bf16[32,16,512]{2,1,0:T(8,128)(2,1)S(1)}, u32[]{:S(2)}, u32[]{:S(2)}) async-start(bf16[32,16,512]{2,1,0:T(8,128)(2,1)} %bitcast.100), calls=%async_computation.4 | async-start | bytes 1048576 | tf_op jit(solution)/shard_map/all_to_all | solution.py:55
